TPU v7x, 512 devices: a whole 4x8x8 slice. The times are simulated.
512 devices in a mesh: gx: 16 (over y_lo, z), gy: 8 (over y_hi, core), rep: 4 (over x).
Axes of the slice: x: 4, y: 8 (y_hi: 4, y_lo: 2; y = y_hi * 2 + y_lo), z: 8, core: 2. Of those that a mesh axis runs over, the one named last changes fastest.
Arguments:
- positions: float32 [4, 3, 256, 16384], P('rep', None, 'gx', 'gy'), may hold values from 0 to 4
- velocities: float32 [4, 3, 256, 16384], P('rep', None, 'gx', 'gy'), may hold values from -6 to 6
- noise: float32 [4, 3, 256, 16384], P('rep', None, 'gx', 'gy'), may hold values from -6 to 6
- bonds: int32 [256, 256, 8], P('gx', 'gy'), may hold values from 0 to 1, as said below
Outputs:
- mean_force: float32 [3, 256, 16384], P(None, 'gx', 'gy')
- new_velocity: float32 [4, 3, 256, 16384], P('rep', None, 'gx', 'gy')
- new_position: float32 [4, 3, 256, 16384], P('rep', None, 'gx', 'gy')
Inputs may be any that keep to these rules, and one draw needn't show every extreme that they name: bonds is symmetric: bonds of cluster c for offset k equals bonds of cluster c + offset k for the opposite offset k + 4 (k < 4); entries for neighbours outside the grid are 0.
All inputs are finite; a program needn't handle non-finite values.
Results may differ from a plain program's by a relative error of at most 0.0001.
Values sent between devices are 32-bit elements; how exact they have to be, the bound alone decides.
No kernel may reach another device: no remote copies, remote signals or barrier semaphores. Data moves between devices by JAX's collectives and lax.ppermute only.
A program may use at most 64 MiB of HBM per device.

v0:
```python
import jax
import jax.numpy as jnp
from jax import lax
from jax.sharding import PartitionSpec as P

ATOMS = 64


spacing = 4.0
friction = 0.6
noise_coef = 0.8
time_step = 0.2
offsets_list = ((0, 1), (1, -1), (1, 0), (1, 1), (0, -1), (-1, 1), (-1, 0), (-1, -1))


def passed_along(value, axis, steps):
    count = lax.axis_size(axis)
    leading, last = (max(0, -steps), min(count, count - steps))
    return lax.ppermute(value, axis, [(source, source + steps) for source in range(leading, last)])


def pair_weight(squared):
    return 2.0 * jnp.exp(-2.0 * squared) - 0.5 * jnp.exp(-0.5 * squared)


def tile_forces(own_atoms, neighbour, flag_col, shift_x, shift_y):
    shift_vec = jnp.array([shift_x * spacing, shift_y * spacing, 0.0], jnp.float32)[:, None, None]
    moved_atoms = neighbour + shift_vec
    differ = own_atoms[:, :, :, None] - moved_atoms[:, :, None, :]
    squared = jnp.sum(differ * differ, axis=0)
    weighted = (pair_weight(squared) * flag_col[:, None, None])[None] * differ
    return (jnp.sum(weighted, axis=3), -jnp.sum(weighted, axis=2))


def pad_cols(values, before, after):
    return jnp.pad(values, ((0, 0), (before, after), (0, 0)))


def per_device(positions, velocities, noise, bonds):
    rows_local = positions.shape[2]
    cols_local = positions.shape[3] // ATOMS
    coords = positions[0].reshape(3, rows_local, cols_local, ATOMS)
    lower_col = passed_along(coords[:, :, cols_local - 1 : cols_local], "gy", 1)
    upper_col = passed_along(coords[:, :, 0:1], "gy", -1)
    widened = jnp.concatenate([lower_col, coords, upper_col], axis=2)
    next_rows = passed_along(widened[:, 0:1], "gx", -1)
    flag_all = bonds.astype(jnp.float32)
    ones_flag = jnp.ones((cols_local,), jnp.float32)
    extended = jnp.concatenate([widened, next_rows], axis=1)

    def half_row(row_index):
        window = lax.dynamic_slice_in_dim(extended, row_index, 2, 1)
        own_atoms = window[:, 0, 1 : cols_local + 1]
        flag_row = lax.dynamic_index_in_dim(flag_all, row_index, 0, keepdims=False)
        self_part = tile_forces(own_atoms, own_atoms, ones_flag, 0, 0)[0]
        side_own, side_other = tile_forces(
            own_atoms, window[:, 0, 2 : cols_local + 2], flag_row[:, 0], 0, 1
        )
        same_row = pad_cols(self_part + side_own, 1, 1) + pad_cols(side_other, 2, 0)
        next_part = jnp.zeros((3, cols_local + 2, ATOMS), jnp.float32)
        for offset_index in (1, 2, 3):
            shift_y = offsets_list[offset_index][1]
            neighbour = window[:, 1, 1 + shift_y : 1 + shift_y + cols_local]
            part_own, part_other = tile_forces(
                own_atoms, neighbour, flag_row[:, offset_index], 1, shift_y
            )
            same_row = same_row + pad_cols(part_own, 1, 1)
            next_part = next_part + pad_cols(part_other, 1 + shift_y, 1 - shift_y)
        return (same_row, next_part)

    same_rows, next_parts = lax.map(half_row, jnp.arange(rows_local, dtype=jnp.int32))
    same_rows = jnp.transpose(same_rows, (1, 0, 2, 3))
    next_parts = jnp.transpose(next_parts, (1, 0, 2, 3))
    zero_pad = ((0, 0), (0, 1), (0, 0), (0, 0))
    ghost_force = jnp.pad(same_rows, zero_pad) + jnp.pad(
        next_parts, ((0, 0), (1, 0), (0, 0), (0, 0))
    )
    returned_row = passed_along(ghost_force[:, rows_local : rows_local + 1], "gx", 1)
    domain_force = ghost_force[:, :rows_local] + jnp.pad(
        returned_row, ((0, 0), (0, rows_local - 1), (0, 0), (0, 0))
    )
    from_upper = passed_along(domain_force[:, :, 0:1], "gy", -1)
    from_lower = passed_along(domain_force[:, :, cols_local + 1 : cols_local + 2], "gy", 1)
    own_force = domain_force[:, :, 1 : cols_local + 1]
    own_force = own_force + jnp.pad(from_lower, ((0, 0), (0, 0), (0, cols_local - 1), (0, 0)))
    own_force = own_force + jnp.pad(from_upper, ((0, 0), (0, 0), (cols_local - 1, 0), (0, 0)))
    summed_force = lax.psum(own_force, "rep")
    mean_force = (summed_force / lax.axis_size("rep")).reshape(3, rows_local, cols_local * ATOMS)
    new_velocity = friction * velocities + time_step * mean_force[None] + noise_coef * noise
    new_position = positions + time_step * new_velocity
    return (mean_force, new_velocity, new_position)


def solution(mesh):
    in_specs = (
        P("rep", None, "gx", "gy"),
        P("rep", None, "gx", "gy"),
        P("rep", None, "gx", "gy"),
        P("gx", "gy", None),
    )
    out_specs = (P(None, "gx", "gy"), P("rep", None, "gx", "gy"), P("rep", None, "gx", "gy"))
    return jax.shard_map(
        per_device, mesh=mesh, in_specs=in_specs, out_specs=out_specs, check_vma=False
    )
```

profile of v0, /device:TPU:16, one launch (start us, length us, event | category | flops | bytes accessed | tf_op | source)
XLA Modules:
  0.0 383.9 jit_solution(1527822464493937966)
XLA Ops:
  10.5 4.5 %collective-permute-start.1 = (f32[3,16,1,64]{3,2,1,0:T(1,128)S(1)}, f32[3,16,1,64]{3,2,1,0:T(1,128)S(1)}, u32[]{:S(2)}, u32[]{:S(2)}) collective-permute-start(f32[3,16,1,64]{3,2,1,0:T(1,128)S(1)} %get-tuple-element.225), channel_id=1, source_target_pairs={{4,0},{8,4},{12,8},{16,12},{20,16},{24,20},{28,24},{5,1},{9,5},{13... | collective-permute-start | bytes 36872 | tf_op jit(solution)/shard_map/ppermute | solution.py:19
  18.5 5.1 %collective-permute-done.2 = f32[3,1,34,64]{3,2,1,0:T(8,128)S(1)} collective-permute-done((f32[3,1,34,64]{3,2,1,0:T(8,128)S(1)}, f32[3,1,34,64]{3,2,1,0:T(8,128)S(1)}, u32[]{:S(2)}, u32[]{:S(2)}) %collective-permute-start.2) | collective-permute-done | bytes 26144 | tf_op jit(solution)/shard_map/ppermute | solution.py:19
  23.9 267.5 %while.15 = (s32[]{:T(128)}, f32[16,3,34,64]{3,2,1,0:T(8,128)}, f32[16,3,34,64]{3,2,1,0:T(8,128)}, s32[16]{0:T(128)S(1)}, f32[3,17,34,64]{3,2,1,0:T(8,128)S(1)},...) while((s32[]{:T(128)}, f32[16,3,34,64]{3,2,1,0:T(8,128)}, ...), condition=%wide.region_15.16_spmd.clone, body=%wide.region_0.15_spmd.sunk.clone.sunk | while | flops 16554250 | bytes 15368580 | solution.py:71
  31.7 4.4 %fusion.31 = (f32[3,32,64]{2,1,0:T(8,128)S(1)}, f32[3,32,64]{2,1,0:T(8,128)S(1)}, f32[32,64,64]{2,1,0:T(8,128)S(1)}, f32[32,64,64]{2,1,0:T(8,128)S(1)}, f32[3,32...) fusion(f32[32,64,64]{2,1,0:T(8,128)S(1)} %subtract_multiply_fusion.18, ...), kind=kLoop, calls=%fused_computation.12.clone.1 | loop fusion | flops 6391808 | bytes 2867200 | tf_op jit(solution)/shard_map/while/body/eval_jaxpr/reduce_sum | solution.py:32
  48.5 4.4 %fusion.31 = (f32[3,32,64]{2,1,0:T(8,128)S(1)}, f32[3,32,64]{2,1,0:T(8,128)S(1)}, f32[32,64,64]{2,1,0:T(8,128)S(1)}, f32[32,64,64]{2,1,0:T(8,128)S(1)}, f32[3,32...) fusion(f32[32,64,64]{2,1,0:T(8,128)S(1)} %subtract_multiply_fusion.18, ...), kind=kLoop, calls=%fused_computation.12.clone.1 | loop fusion | flops 6391808 | bytes 2867200 | tf_op jit(solution)/shard_map/while/body/eval_jaxpr/reduce_sum | solution.py:32
  53.5 3.0 fusion.32
  65.1 4.4 %fusion.31 = (f32[3,32,64]{2,1,0:T(8,128)S(1)}, f32[3,32,64]{2,1,0:T(8,128)S(1)}, f32[32,64,64]{2,1,0:T(8,128)S(1)}, f32[32,64,64]{2,1,0:T(8,128)S(1)}, f32[3,32...) fusion(f32[32,64,64]{2,1,0:T(8,128)S(1)} %subtract_multiply_fusion.18, ...), kind=kLoop, calls=%fused_computation.12.clone.1 | loop fusion | flops 6391808 | bytes 2867200 | tf_op jit(solution)/shard_map/while/body/eval_jaxpr/reduce_sum | solution.py:32
  81.9 4.4 %fusion.31 = (f32[3,32,64]{2,1,0:T(8,128)S(1)}, f32[3,32,64]{2,1,0:T(8,128)S(1)}, f32[32,64,64]{2,1,0:T(8,128)S(1)}, f32[32,64,64]{2,1,0:T(8,128)S(1)}, f32[3,32...) fusion(f32[32,64,64]{2,1,0:T(8,128)S(1)} %subtract_multiply_fusion.18, ...), kind=kLoop, calls=%fused_computation.12.clone.1 | loop fusion | flops 6391808 | bytes 2867200 | tf_op jit(solution)/shard_map/while/body/eval_jaxpr/reduce_sum | solution.py:32
  87.0 3.0 fusion.32
  98.6 4.4 %fusion.31 = (f32[3,32,64]{2,1,0:T(8,128)S(1)}, f32[3,32,64]{2,1,0:T(8,128)S(1)}, f32[32,64,64]{2,1,0:T(8,128)S(1)}, f32[32,64,64]{2,1,0:T(8,128)S(1)}, f32[3,32...) fusion(f32[32,64,64]{2,1,0:T(8,128)S(1)} %subtract_multiply_fusion.18, ...), kind=kLoop, calls=%fused_computation.12.clone.1 | loop fusion | flops 6391808 | bytes 2867200 | tf_op jit(solution)/shard_map/while/body/eval_jaxpr/reduce_sum | solution.py:32
  103.7 3.0 fusion.32
  115.3 4.4 %fusion.31 = (f32[3,32,64]{2,1,0:T(8,128)S(1)}, f32[3,32,64]{2,1,0:T(8,128)S(1)}, f32[32,64,64]{2,1,0:T(8,128)S(1)}, f32[32,64,64]{2,1,0:T(8,128)S(1)}, f32[3,32...) fusion(f32[32,64,64]{2,1,0:T(8,128)S(1)} %subtract_multiply_fusion.18, ...), kind=kLoop, calls=%fused_computation.12.clone.1 | loop fusion | flops 6391808 | bytes 2867200 | tf_op jit(solution)/shard_map/while/body/eval_jaxpr/reduce_sum | solution.py:32
  120.4 3.0 fusion.32
  132.0 4.4 %fusion.31 = (f32[3,32,64]{2,1,0:T(8,128)S(1)}, f32[3,32,64]{2,1,0:T(8,128)S(1)}, f32[32,64,64]{2,1,0:T(8,128)S(1)}, f32[32,64,64]{2,1,0:T(8,128)S(1)}, f32[3,32...) fusion(f32[32,64,64]{2,1,0:T(8,128)S(1)} %subtract_multiply_fusion.18, ...), kind=kLoop, calls=%fused_computation.12.clone.1 | loop fusion | flops 6391808 | bytes 2867200 | tf_op jit(solution)/shard_map/while/body/eval_jaxpr/reduce_sum | solution.py:32
  137.1 3.0 fusion.32
  148.8 4.4 %fusion.31 = (f32[3,32,64]{2,1,0:T(8,128)S(1)}, f32[3,32,64]{2,1,0:T(8,128)S(1)}, f32[32,64,64]{2,1,0:T(8,128)S(1)}, f32[32,64,64]{2,1,0:T(8,128)S(1)}, f32[3,32...) fusion(f32[32,64,64]{2,1,0:T(8,128)S(1)} %subtract_multiply_fusion.18, ...), kind=kLoop, calls=%fused_computation.12.clone.1 | loop fusion | flops 6391808 | bytes 2867200 | tf_op jit(solution)/shard_map/while/body/eval_jaxpr/reduce_sum | solution.py:32
  153.8 3.0 fusion.32
  165.5 4.4 %fusion.31 = (f32[3,32,64]{2,1,0:T(8,128)S(1)}, f32[3,32,64]{2,1,0:T(8,128)S(1)}, f32[32,64,64]{2,1,0:T(8,128)S(1)}, f32[32,64,64]{2,1,0:T(8,128)S(1)}, f32[3,32...) fusion(f32[32,64,64]{2,1,0:T(8,128)S(1)} %subtract_multiply_fusion.18, ...), kind=kLoop, calls=%fused_computation.12.clone.1 | loop fusion | flops 6391808 | bytes 2867200 | tf_op jit(solution)/shard_map/while/body/eval_jaxpr/reduce_sum | solution.py:32
  170.5 3.0 fusion.32
  182.1 4.4 %fusion.31 = (f32[3,32,64]{2,1,0:T(8,128)S(1)}, f32[3,32,64]{2,1,0:T(8,128)S(1)}, f32[32,64,64]{2,1,0:T(8,128)S(1)}, f32[32,64,64]{2,1,0:T(8,128)S(1)}, f32[3,32...) fusion(f32[32,64,64]{2,1,0:T(8,128)S(1)} %subtract_multiply_fusion.18, ...), kind=kLoop, calls=%fused_computation.12.clone.1 | loop fusion | flops 6391808 | bytes 2867200 | tf_op jit(solution)/shard_map/while/body/eval_jaxpr/reduce_sum | solution.py:32
  187.2 3.0 fusion.32
  198.9 4.4 %fusion.31 = (f32[3,32,64]{2,1,0:T(8,128)S(1)}, f32[3,32,64]{2,1,0:T(8,128)S(1)}, f32[32,64,64]{2,1,0:T(8,128)S(1)}, f32[32,64,64]{2,1,0:T(8,128)S(1)}, f32[3,32...) fusion(f32[32,64,64]{2,1,0:T(8,128)S(1)} %subtract_multiply_fusion.18, ...), kind=kLoop, calls=%fused_computation.12.clone.1 | loop fusion | flops 6391808 | bytes 2867200 | tf_op jit(solution)/shard_map/while/body/eval_jaxpr/reduce_sum | solution.py:32
  204.0 3.0 fusion.32
  215.6 4.4 %fusion.31 = (f32[3,32,64]{2,1,0:T(8,128)S(1)}, f32[3,32,64]{2,1,0:T(8,128)S(1)}, f32[32,64,64]{2,1,0:T(8,128)S(1)}, f32[32,64,64]{2,1,0:T(8,128)S(1)}, f32[3,32...) fusion(f32[32,64,64]{2,1,0:T(8,128)S(1)} %subtract_multiply_fusion.18, ...), kind=kLoop, calls=%fused_computation.12.clone.1 | loop fusion | flops 6391808 | bytes 2867200 | tf_op jit(solution)/shard_map/while/body/eval_jaxpr/reduce_sum | solution.py:32
  220.7 3.0 fusion.32
  232.3 4.4 %fusion.31 = (f32[3,32,64]{2,1,0:T(8,128)S(1)}, f32[3,32,64]{2,1,0:T(8,128)S(1)}, f32[32,64,64]{2,1,0:T(8,128)S(1)}, f32[32,64,64]{2,1,0:T(8,128)S(1)}, f32[3,32...) fusion(f32[32,64,64]{2,1,0:T(8,128)S(1)} %subtract_multiply_fusion.18, ...), kind=kLoop, calls=%fused_computation.12.clone.1 | loop fusion | flops 6391808 | bytes 2867200 | tf_op jit(solution)/shard_map/while/body/eval_jaxpr/reduce_sum | solution.py:32
  249.0 4.4 %fusion.31 = (f32[3,32,64]{2,1,0:T(8,128)S(1)}, f32[3,32,64]{2,1,0:T(8,128)S(1)}, f32[32,64,64]{2,1,0:T(8,128)S(1)}, f32[32,64,64]{2,1,0:T(8,128)S(1)}, f32[3,32...) fusion(f32[32,64,64]{2,1,0:T(8,128)S(1)} %subtract_multiply_fusion.18, ...), kind=kLoop, calls=%fused_computation.12.clone.1 | loop fusion | flops 6391808 | bytes 2867200 | tf_op jit(solution)/shard_map/while/body/eval_jaxpr/reduce_sum | solution.py:32
  265.7 4.4 %fusion.31 = (f32[3,32,64]{2,1,0:T(8,128)S(1)}, f32[3,32,64]{2,1,0:T(8,128)S(1)}, f32[32,64,64]{2,1,0:T(8,128)S(1)}, f32[32,64,64]{2,1,0:T(8,128)S(1)}, f32[3,32...) fusion(f32[32,64,64]{2,1,0:T(8,128)S(1)} %subtract_multiply_fusion.18, ...), kind=kLoop, calls=%fused_computation.12.clone.1 | loop fusion | flops 6391808 | bytes 2867200 | tf_op jit(solution)/shard_map/while/body/eval_jaxpr/reduce_sum | solution.py:32
  282.4 4.4 %fusion.31 = (f32[3,32,64]{2,1,0:T(8,128)S(1)}, f32[3,32,64]{2,1,0:T(8,128)S(1)}, f32[32,64,64]{2,1,0:T(8,128)S(1)}, f32[32,64,64]{2,1,0:T(8,128)S(1)}, f32[3,32...) fusion(f32[32,64,64]{2,1,0:T(8,128)S(1)} %subtract_multiply_fusion.18, ...), kind=kLoop, calls=%fused_computation.12.clone.1 | loop fusion | flops 6391808 | bytes 2867200 | tf_op jit(solution)/shard_map/while/body/eval_jaxpr/reduce_sum | solution.py:32
  292.2 4.3 %collective-permute-start.3 = (f32[3,1,34,64]{3,2,0,1:T(8,128)S(1)}, f32[3,1,34,64]{3,2,0,1:T(8,128)S(1)}, u32[]{:S(2)}, u32[]{:S(2)}) collective-permute-start(f32[3,1,34,64]{3,2,0,1:T(8,128)S(1)} %pad_add_fusion), channel_id=1, source_target_pairs={{0,32},{32,64},{64,96},{96,128},{128,160},{160,192},{192,224},{224... | collective-permute-start | bytes 78344 | tf_op jit(solution)/shard_map/ppermute | solution.py:19
  300.0 5.1 %collective-permute-start.4 = (f32[3,16,1,64]{3,2,0,1:T(1,128)S(1)}, f32[3,16,1,64]{3,2,0,1:T(1,128)S(1)}, u32[]{:S(2)}, u32[]{:S(2)}) collective-permute-start(f32[3,16,1,64]{3,2,0,1:T(1,128)S(1)} %get-tuple-element.220), channel_id=1, source_target_pairs={{0,4},{4,8},{8,12},{12,16},{16,20},{20,24},{24,28},{1,5},{5,9},{9,... | collective-permute-start | bytes 36872 | tf_op jit(solution)/shard_map/ppermute | solution.py:19
  310.2 62.5 %all-reduce.15.cloned.1.call-done = f32[3,16,32,64]{3,2,0,1:T(8,128)} async-done(((f32[3,16,32,64]{3,2,0,1:T(8,128)}), f32[3,16,32,64]{3,2,0,1:T(8,128)}) %all-reduce.15.cloned.1.call-update) | async-done | bytes 393232 | tf_op jit(solution)/shard_map/psum | solution.py:87
  (385 shorter events, 134.1 us)
Async XLA Ops:
  7.2 11.4 %copy-start.5 = (s32[16,32,8]{1,2,0:T(8,128)S(1)}, s32[16,32,8]{1,2,0:T(8,128)}, u32[]{:S(2)}) copy-start(s32[16,32,8]{1,2,0:T(8,128)} %param.14) | copy-start | bytes 49156
  7.2 365.6 %all-reduce.15.cloned.1.call-start = ((), (), s32[]{:S(2)}) async-start(), calls=%async_computation | async-start | bytes 1572864 | tf_op jit(solution)/shard_map/psum | solution.py:87
  8.6 6.5 %collective-permute-start = (f32[3,16,1,64]{3,2,1,0:T(1,128)S(1)}, f32[3,16,1,64]{3,2,1,0:T(1,128)S(1)}, u32[]{:S(2)}, u32[]{:S(2)}) collective-permute-start(f32[3,16,1,64]{3,2,1,0:T(1,128)S(1)} %get-tuple-element.224), channel_id=1, source_target_pairs={{0,4},{4,8},{8,12},{12,16},{16,20},{20,24},{24,28},{1,5},{5,9},{9,... | collective-permute-start | bytes 36872 | tf_op jit(solution)/shard_map/ppermute | solution.py:19
  10.5 6.5 %collective-permute-start.1 = (f32[3,16,1,64]{3,2,1,0:T(1,128)S(1)}, f32[3,16,1,64]{3,2,1,0:T(1,128)S(1)}, u32[]{:S(2)}, u32[]{:S(2)}) collective-permute-start(f32[3,16,1,64]{3,2,1,0:T(1,128)S(1)} %get-tuple-element.225), channel_id=1, source_target_pairs={{4,0},{8,4},{12,8},{16,12},{20,16},{24,20},{28,24},{5,1},{9,5},{13... | collective-permute-start | bytes 36872 | tf_op jit(solution)/shard_map/ppermute | solution.py:19
  17.0 6.8 %copy-start.6 = (f32[3]{0:T(128)S(1)}, f32[3]{0:T(128)}, u32[]{:S(2)}) copy-start(f32[3]{0:T(128)} %constant.85.clone..sunk.2) | copy-start | bytes 40
  17.0 6.8 %copy-start.7 = (f32[3]{0:T(128)S(1)}, f32[3]{0:T(128)}, u32[]{:S(2)}) copy-start(f32[3]{0:T(128)} %constant.86.clone..sunk.2) | copy-start | bytes 40
  17.0 6.8 %copy-start.8 = (f32[3]{0:T(128)S(1)}, f32[3]{0:T(128)}, u32[]{:S(2)}) copy-start(f32[3]{0:T(128)} %constant.87.clone..sunk.2) | copy-start | bytes 40
  17.1 6.8 %copy-start.9 = (f32[3]{0:T(128)S(1)}, f32[3]{0:T(128)}, u32[]{:S(2)}) copy-start(f32[3]{0:T(128)} %constant.88.clone..sunk.2) | copy-start | bytes 40
  17.1 6.6 %collective-permute-start.2 = (f32[3,1,34,64]{3,2,1,0:T(8,128)S(1)}, f32[3,1,34,64]{3,2,1,0:T(8,128)S(1)}, u32[]{:S(2)}, u32[]{:S(2)}) collective-permute-start(f32[3,1,34,64]{3,2,1,0:T(8,128)S(1)} %pad_maximum_fusion.1), channel_id=1, source_target_pairs={{32,0},{64,32},{96,64},{128,96},{160,128},{192,160},{224,192},{256... | collective-permute-start | bytes 78344 | tf_op jit(solution)/shard_map/ppermute | solution.py:19
  23.9 2.7 copy-start
  36.8 3.8 copy-start.1
  53.5 3.8 copy-start.1
  57.3 2.7 copy-start
  70.2 3.8 copy-start.1
  74.1 2.7 copy-start
  87.0 3.8 copy-start.1
  103.7 3.8 copy-start.1
  107.5 2.7 copy-start
  120.4 3.8 copy-start.1
  137.1 3.8 %copy-start.1 = (f32[3,17,34,64]{3,2,1,0:T(8,128)S(1)}, f32[3,17,34,64]{3,2,1,0:T(8,128)}, u32[]{:S(2)}) copy-start(f32[3,17,34,64]{3,2,1,0:T(8,128)} %copy-done) | copy-start | bytes 1331716 | tf_op jit(solution)/shard_map/while
  153.8 3.8 copy-start.1
  170.5 3.8 copy-start.1
  187.2 3.8 copy-start.1
  204.0 3.8 copy-start.1
  220.7 3.8 copy-start.1
  237.4 3.8 copy-start.1
  254.1 3.8 copy-start.1
  270.8 3.8 copy-start.1
  287.5 3.8 copy-start.1
  292.2 6.1 %collective-permute-start.3 = (f32[3,1,34,64]{3,2,0,1:T(8,128)S(1)}, f32[3,1,34,64]{3,2,0,1:T(8,128)S(1)}, u32[]{:S(2)}, u32[]{:S(2)}) collective-permute-start(f32[3,1,34,64]{3,2,0,1:T(8,128)S(1)} %pad_add_fusion), channel_id=1, source_target_pairs={{0,32},{32,64},{64,96},{96,128},{128,160},{160,192},{192,224},{224... | collective-permute-start | bytes 78344 | tf_op jit(solution)/shard_map/ppermute | solution.py:19
  300.0 7.1 %collective-permute-start.4 = (f32[3,16,1,64]{3,2,0,1:T(1,128)S(1)}, f32[3,16,1,64]{3,2,0,1:T(1,128)S(1)}, u32[]{:S(2)}, u32[]{:S(2)}) collective-permute-start(f32[3,16,1,64]{3,2,0,1:T(1,128)S(1)} %get-tuple-element.220), channel_id=1, source_target_pairs={{0,4},{4,8},{8,12},{12,16},{16,20},{20,24},{24,28},{1,5},{5,9},{9,... | collective-permute-start | bytes 36872 | tf_op jit(solution)/shard_map/ppermute | solution.py:19
  305.1 4.1 %collective-permute-start.5 = (f32[3,16,1,64]{3,2,0,1:T(1,128)S(1)}, f32[3,16,1,64]{3,2,0,1:T(1,128)S(1)}, u32[]{:S(2)}, u32[]{:S(2)}) collective-permute-start(f32[3,16,1,64]{3,2,0,1:T(1,128)S(1)} %get-tuple-element.221), channel_id=1, source_target_pairs={{4,0},{8,4},{12,8},{16,12},{20,16},{24,20},{28,24},{5,1},{9,5},{13... | collective-permute-start | bytes 36872 | tf_op jit(solution)/shard_map/ppermute | solution.py:19
  (15 other events, 36.6 us)
Sparse Core Ops, SparseCore 0:
  310.3 62.3 all-reduce.14
where the time goes:
time: 385 us; the launch traced here: 384 us
  other arithmetic  208 us (54%)
  waiting for transfers between devices  73.6 us (19%)
  loops' own time  54 us (14%)
  starting transfers between devices  19.2 us (5%)
  local copies, waits for them, and re-layouts  14.4 us (4%)
  between operations  14.3 us (4%)
    reduce_sum x32, other arithmetic, tile_forces(): return (jnp.sum(weighted, axis=3), -jnp.sum(weighted, axis=2))  118 us
    psum x1, waiting for transfers between devices, per_device(): summed_force = lax.psum(own_force, 'rep')  62.5 us
    another operation x1, loops' own time, per_device(): lax.map(half_row, jnp.arange(rows_local, dtype=jnp.int32))  54 us
    reduce_sum x16, other arithmetic, tile_forces(): squared = jnp.sum(differ * differ, axis=0)  43.4 us
    mul x64, other arithmetic, tile_forces(): weighted = (pair_weight(squared) * flag_col[:, None, None])[None] * differ  22.3 us
    ppermute x6, starting transfers between devices, passed_along(): lax.ppermute(value, axis, [(source, source + steps) for source in range(l...  19.2 us
    dynamic_update_slice x16, other arithmetic, per_device(): lax.map(half_row, jnp.arange(rows_local, dtype=jnp.int32))  11.5 us
    ppermute x6, waiting for transfers between devices, passed_along(): lax.ppermute(value, axis, [(source, source + steps) for source in range(l...  11 us
  transfers between devices with their start and end apart: 7, of which 5 were waited for; matrix products, arithmetic and copies ran while one was open for 0% of the time, Pallas kernels for 0%

commit v1 on v0

v1 whole, which is shorter than its diff:
```python
import jax
import jax.numpy as jnp
from jax import lax
from jax.experimental import pallas as pl
from jax.experimental.pallas import tpu as pltpu
from jax.sharding import PartitionSpec as P

ATOMS = 64


spacing = 4.0
friction = 0.6
noise_coef = 0.8
time_step = 0.2
offsets_list = ((0, 1), (1, -1), (1, 0), (1, 1), (0, -1), (-1, 1), (-1, 0), (-1, -1))
LANES = 128


def passed_along(value, axis, steps):
    count = lax.axis_size(axis)
    leading, last = (max(0, -steps), min(count, count - steps))
    return lax.ppermute(value, axis, [(source, source + steps) for source in range(leading, last)])


def ring_shift(value, axis, steps):
    count = lax.axis_size(axis)
    return lax.ppermute(value, axis, [(source, (source + steps) % count) for source in range(count)])


def force_kernel(rows, pairs, chunks, own_ref, halo_ref, flag_ref, out_ref, cbuf):
    n_blocks = 2 * pairs + 1
    left = lax.broadcasted_iota(jnp.int32, (ATOMS, LANES), 1) < ATOMS

    def build(h, slot):
        for c in range(3):
            prev = None
            for t in range(chunks):
                if 2 * t - 1 >= n_blocks:
                    break
                r = halo_ref[h, c : c + 1, t * LANES : (t + 1) * LANES]
                tt = jnp.transpose(jnp.broadcast_to(r, (LANES, LANES)))
                if prev is not None and 2 * t - 1 < n_blocks:
                    cbuf[slot, c, 2 * t - 1] = jnp.where(left, prev[ATOMS:], tt[:ATOMS])
                if 2 * t < n_blocks:
                    cbuf[slot, c, 2 * t] = jnp.where(left, tt[:ATOMS], tt[ATOMS:])
                prev = tt

    build(0, 0)
    build(1, 1)

    offsets = ((0, 0),) + offsets_list

    def row_body(i, carry):
        build(i + 2, lax.rem(i + 2, 3))

        def pair_body(k, carry2):
            base = pl.multiple_of(k * LANES, LANES)
            own = own_ref[i, :, pl.ds(base, LANES)]
            flags = flag_ref[i, :, pl.ds(base, LANES)]
            acc = [jnp.zeros((8, LANES), jnp.float32) for _ in range(3)]
            for oi, (dx, dy) in enumerate(offsets):
                slot = lax.rem(i + 1 + dx, 3)
                n = 2 * k + 1 + dy
                if oi == 0:
                    f2 = jnp.full((8, LANES), 2.0, jnp.float32)
                    fh = jnp.full((8, LANES), 0.5, jnp.float32)
                else:
                    f = jnp.broadcast_to(flags[oi - 1 : oi], (8, LANES))
                    f2 = 2.0 * f
                    fh = 0.5 * f
                xs = jnp.broadcast_to(own[0:1] - dx * spacing, (8, LANES))
                ys = jnp.broadcast_to(own[1:2] - dy * spacing, (8, LANES))
                zs = jnp.broadcast_to(own[2:3], (8, LANES))
                for r in range(ATOMS // 8):
                    cx = cbuf[slot, 0, n, r * 8 : (r + 1) * 8, :]
                    cy = cbuf[slot, 1, n, r * 8 : (r + 1) * 8, :]
                    cz = cbuf[slot, 2, n, r * 8 : (r + 1) * 8, :]
                    ddx = xs - cx
                    ddy = ys - cy
                    ddz = zs - cz
                    s = ddx * ddx + ddy * ddy + ddz * ddz
                    a = jnp.exp(-0.5 * s)
                    a2 = a * a
                    w = f2 * (a2 * a2) - fh * a
                    acc[0] = acc[0] + w * ddx
                    acc[1] = acc[1] + w * ddy
                    acc[2] = acc[2] + w * ddz
            for c in range(3):
                out_ref[i, c : c + 1, pl.ds(base, LANES)] = jnp.sum(acc[c], axis=0, keepdims=True)
            return carry2

        lax.fori_loop(0, pairs, pair_body, 0)
        return carry

    lax.fori_loop(0, rows, row_body, 0)


def cluster_forces(own, halo, flags):
    rows, _, width = own.shape
    pairs = width // LANES
    chunks = halo.shape[2] // LANES
    n_blocks = 2 * pairs + 1
    kernel = lambda *refs: force_kernel(rows, pairs, chunks, *refs)
    pair_count = rows * pairs * 9 * ATOMS * LANES
    return pl.pallas_call(
        kernel,
        out_shape=jax.ShapeDtypeStruct(own.shape, jnp.float32),
        in_specs=[pl.BlockSpec(memory_space=pltpu.VMEM)] * 3,
        out_specs=pl.BlockSpec(memory_space=pltpu.VMEM),
        scratch_shapes=[pltpu.VMEM((3, 3, n_blocks, ATOMS, LANES), jnp.float32)],
        compiler_params=pltpu.CompilerParams(vmem_limit_bytes=48 * 1024 * 1024),
        cost_estimate=pl.CostEstimate(
            flops=20 * pair_count,
            transcendentals=pair_count,
            bytes_accessed=4 * (own.size * 2 + halo.size + flags.size),
        ),
    )(own, halo, flags)


def per_device(positions, velocities, noise, bonds):
    rows_local = positions.shape[2]
    cols_local = positions.shape[3] // ATOMS
    width = cols_local * ATOMS
    coords = positions[0]
    lower_col = passed_along(coords[:, :, width - ATOMS :], "gy", 1)
    upper_col = passed_along(coords[:, :, :ATOMS], "gy", -1)
    widened = jnp.concatenate([lower_col, coords, upper_col], axis=2)
    prev_row = passed_along(widened[:, rows_local - 1 :], "gx", 1)
    next_row = passed_along(widened[:, :1], "gx", -1)
    halo = jnp.concatenate([prev_row, widened, next_row], axis=1)
    chunks = -(-(width + 2 * ATOMS) // LANES)
    halo = jnp.pad(halo, ((0, 0), (0, 0), (0, chunks * LANES - width - 2 * ATOMS)))
    halo = jnp.transpose(halo, (1, 0, 2))
    own = jnp.transpose(coords, (1, 0, 2))
    flags = jnp.repeat(jnp.transpose(bonds.astype(jnp.float32), (0, 2, 1)), ATOMS, axis=2)
    force = jnp.transpose(cluster_forces(own, halo, flags), (1, 0, 2))
    across = ring_shift(force, "rep", 2)
    near = ring_shift(force, "rep", 1)
    far = ring_shift(force, "rep", 3)
    summed_force = (force + across) + (near + far)
    mean_force = summed_force / lax.axis_size("rep")
    new_velocity = friction * velocities + time_step * mean_force[None] + noise_coef * noise
    new_position = positions + time_step * new_velocity
    return (mean_force, new_velocity, new_position)


def solution(mesh):
    in_specs = (
        P("rep", None, "gx", "gy"),
        P("rep", None, "gx", "gy"),
        P("rep", None, "gx", "gy"),
        P("gx", "gy", None),
    )
    out_specs = (P(None, "gx", "gy"), P("rep", None, "gx", "gy"), P("rep", None, "gx", "gy"))
    return jax.shard_map(
        per_device, mesh=mesh, in_specs=in_specs, out_specs=out_specs, check_vma=False
    )
```

time: 385 us -> 144 us (0.37)
  the two profiles are of different devices: /device:TPU:16 before, /device:TPU:26 now
where the time goes in v1:
time: 144 us; the launch traced here: 143 us
  Pallas kernels  80 us (56%)
  starting transfers between devices  26.7 us (19%)
  waiting for transfers between devices  25.2 us (18%)
  local copies, waits for them, and re-layouts  9.08 us (6%)
  other arithmetic  1.61 us (1%)
    pallas_call x1, Pallas kernels, cluster_forces(): pl.pallas_call(kernel, out_shape=jax.ShapeDtypeStruct(own.shape, jnp.floa...  80 us
    ppermute x3, waiting for transfers between devices, ring_shift(): lax.ppermute(value, axis, [(source, (source + steps) % count) for source...  21.2 us
    ppermute x4, starting transfers between devices, passed_along(): lax.ppermute(value, axis, [(source, source + steps) for source in range(l...  16.9 us
    ppermute x3, starting transfers between devices, ring_shift(): lax.ppermute(value, axis, [(source, (source + steps) % count) for source...  9.88 us
    unnamed x12, local copies, waits for them, and re-layouts  4.26 us
    ppermute x4, waiting for transfers between devices, passed_along(): lax.ppermute(value, axis, [(source, source + steps) for source in range(l...  3.95 us
  transfers between devices with their start and end apart: 7, of which 4 were waited for; matrix products, arithmetic and copies ran while one was open for 3% of the time, Pallas kernels for 0%

profile of v1, /device:TPU:26, one launch (start us, length us, event | category | flops | bytes accessed | tf_op | source)
XLA Modules:
  0.0 143.5 jit_solution(6287557242774151867)
XLA Ops:
  0.6 0.0 copy-start.3
  0.6 1.3 copy.25
  1.9 0.1 fusion.3
  2.0 1.9 %collective-permute-start.1 = (f32[3,16,64]{2,0,1:T(4,128)S(1)}, f32[3,16,64]{2,0,1:T(4,128)S(1)}, u32[]{:S(2)}, u32[]{:S(2)}) collective-permute-start(f32[3,16,64]{2,0,1:T(4,128)S(1)} %get-tuple-element.11), channel_id=1, source_target_pairs={{4,0},{8,4},{12,8},{16,12},{20,16},{24,20},{28,24},{5,1},{9,5},{13... | collective-permute-start | bytes 36872 | tf_op jit(solution)/shard_map/ppermute | solution.py:22
  3.9 2.4 %collective-permute-start = (f32[3,16,64]{2,0,1:T(4,128)S(1)}, f32[3,16,64]{2,0,1:T(4,128)S(1)}, u32[]{:S(2)}, u32[]{:S(2)}) collective-permute-start(f32[3,16,64]{2,0,1:T(4,128)S(1)} %get-tuple-element.12), channel_id=1, source_target_pairs={{0,4},{4,8},{8,12},{12,16},{16,20},{20,24},{24,28},{1,5},{5,9},{9,... | collective-permute-start | bytes 36872 | tf_op jit(solution)/shard_map/ppermute | solution.py:22
  6.4 0.0 collective-permute-done.1
  6.4 3.9 %collective-permute-done = f32[3,16,64]{2,0,1:T(4,128)S(1)} collective-permute-done((f32[3,16,64]{2,0,1:T(4,128)S(1)}, f32[3,16,64]{2,0,1:T(4,128)S(1)}, u32[]{:S(2)}, u32[]{:S(2)}) %collective-permute-start) | collective-permute-done | bytes 12320 | tf_op jit(solution)/shard_map/ppermute | solution.py:22
  10.3 0.7 concatenate.6
  11.1 4.3 %collective-permute-start.2 = (f32[3,1,2176]{2,0,1:T(4,128)S(1)}, f32[3,1,2176]{2,0,1:T(4,128)S(1)}, u32[]{:S(2)}, u32[]{:S(2)}) collective-permute-start(f32[3,1,2176]{2,0,1:T(4,128)S(1)} %get-tuple-element.9), channel_id=1, source_target_pairs={{0,32},{32,64},{64,96},{96,128},{128,160},{160,192},{192,224},{224... | collective-permute-start | bytes 78344 | tf_op jit(solution)/shard_map/ppermute | solution.py:22
  15.3 8.3 %collective-permute-start.3 = (f32[3,1,2176]{2,0,1:T(4,128)S(1)}, f32[3,1,2176]{2,0,1:T(4,128)S(1)}, u32[]{:S(2)}, u32[]{:S(2)}) collective-permute-start(f32[3,1,2176]{2,0,1:T(4,128)S(1)} %get-tuple-element.10), channel_id=1, source_target_pairs={{32,0},{64,32},{96,64},{128,96},{160,128},{192,160},{224,192},{256... | collective-permute-start | bytes 78344 | tf_op jit(solution)/shard_map/ppermute | solution.py:22
  23.6 0.0 copy-done.3
  23.6 1.9 %broadcast_in_dim.4 = f32[16,8,32,64]{3,2,1,0:T(8,128)} broadcast(f32[16,8,32]{2,1,0:T(8,128)S(1)} %convert_bitcast_fusion), dimensions={0,1,2} | broadcast | bytes 1064960 | tf_op jit(solution)/shard_map/broadcast_in_dim | solution.py:135
  25.6 2.1 %reshape.10.refs_2_ = f32[16,8,2048]{2,1,0:T(8,128)S(1)} reshape(f32[16,8,32,64]{3,2,1,0:T(8,128)} %broadcast_in_dim.4) | data formatting | bytes 2097152 | tf_op jit(solution)/shard_map/reshape | solution.py:135
  27.7 0.0 collective-permute-done.2
  27.7 0.0 collective-permute-done.3
  27.7 0.1 maximum_bitcast_fusion.refs_1_
  27.8 0.0 copy-start
  27.8 0.0 copy-start.1
  27.9 0.0 copy-start.2
  27.9 80.0 %shard_map.67 = f32[16,3,2048]{2,1,0:T(4,128)S(1)} custom-call(f32[16,3,2048]{2,1,0:T(4,128)S(1)} %bitcast.22, f32[18,3,2176]{2,1,0:T(4,128)S(1)} %maximum_bitcast_fusion.refs_1_, f32[16,8,2048]{2,1,0:T(8,128)S(1)} %reshape.10.refs_2_), custom_call_target="tpu_custom_call" | custom-call | flops 377487360 | bytes 2305024 | tf_op jit(solution)/shard_map/pallas_call | solution.py:105
  107.9 3.4 %collective-permute-start.5 = (f32[3,16,2048]{2,0,1:T(4,128)S(1)}, f32[3,16,2048]{2,0,1:T(4,128)S(1)}, u32[]{:S(2)}, u32[]{:S(2)}) collective-permute-start(f32[3,16,2048]{2,0,1:T(4,128)S(1)} %bitcast.23), channel_id=1, source_target_pairs={{0,1},{1,2},{2,3},{3,0},{4,5},{5,6},{6,7},{7,4},{8,9},{9,10},{10,1... | collective-permute-start | bytes 1179656 | tf_op jit(solution)/shard_map/ppermute | solution.py:27
  111.3 2.4 %collective-permute-start.6 = (f32[3,16,2048]{2,0,1:T(4,128)S(1)}, f32[3,16,2048]{2,0,1:T(4,128)S(1)}, u32[]{:S(2)}, u32[]{:S(2)}) collective-permute-start(f32[3,16,2048]{2,0,1:T(4,128)S(1)} %bitcast.24), channel_id=1, source_target_pairs={{0,3},{1,0},{2,1},{3,2},{4,7},{5,4},{6,5},{7,6},{8,11},{9,8},{10,9... | collective-permute-start | bytes 1179656 | tf_op jit(solution)/shard_map/ppermute | solution.py:27
  113.8 4.0 %collective-permute-start.4 = (f32[3,16,2048]{2,0,1:T(4,128)S(1)}, f32[3,16,2048]{2,0,1:T(4,128)S(1)}, u32[]{:S(2)}, u32[]{:S(2)}) collective-permute-start(f32[3,16,2048]{2,0,1:T(4,128)S(1)} %bitcast.25), channel_id=1, source_target_pairs={{0,2},{1,3},{2,0},{3,1},{4,6},{5,7},{6,4},{7,5},{8,10},{9,11},{10,... | collective-permute-start | bytes 1179656 | tf_op jit(solution)/shard_map/ppermute | solution.py:27
  117.8 6.7 %collective-permute-done.5 = f32[3,16,2048]{2,0,1:T(4,128)S(1)} collective-permute-done((f32[3,16,2048]{2,0,1:T(4,128)S(1)}, f32[3,16,2048]{2,0,1:T(4,128)S(1)}, u32[]{:S(2)}, u32[]{:S(2)}) %collective-permute-start.5) | collective-permute-done | bytes 393248 | tf_op jit(solution)/shard_map/ppermute | solution.py:27
  124.5 2.8 %collective-permute-done.6 = f32[3,16,2048]{2,0,1:T(4,128)S(1)} collective-permute-done((f32[3,16,2048]{2,0,1:T(4,128)S(1)}, f32[3,16,2048]{2,0,1:T(4,128)S(1)}, u32[]{:S(2)}, u32[]{:S(2)}) %collective-permute-start.6) | collective-permute-done | bytes 393248 | tf_op jit(solution)/shard_map/ppermute | solution.py:27
  127.3 11.7 %collective-permute-done.4 = f32[3,16,2048]{2,0,1:T(4,128)S(1)} collective-permute-done((f32[3,16,2048]{2,0,1:T(4,128)S(1)}, f32[3,16,2048]{2,0,1:T(4,128)S(1)}, u32[]{:S(2)}, u32[]{:S(2)}) %collective-permute-start.4) | collective-permute-done | bytes 393248 | tf_op jit(solution)/shard_map/ppermute | solution.py:27
  139.1 0.0 copy-done.1
  139.1 1.3 copy_add_fusion
  140.4 1.0 copy.13
  141.4 1.0 copy.12
  142.4 0.1 broadcast_multiply_fusion
  142.5 1.0 copy.11
  (4 shorter events, 0.0 us)
Async XLA Ops:
  0.6 23.0 %copy-start.3 = (s32[16,32,8]{1,2,0:T(8,128)S(1)}, s32[16,32,8]{1,2,0:T(8,128)}, u32[]{:S(2)}) copy-start(s32[16,32,8]{1,2,0:T(8,128)} %param.7) | copy-start | bytes 49156
  2.0 4.3 %collective-permute-start.1 = (f32[3,16,64]{2,0,1:T(4,128)S(1)}, f32[3,16,64]{2,0,1:T(4,128)S(1)}, u32[]{:S(2)}, u32[]{:S(2)}) collective-permute-start(f32[3,16,64]{2,0,1:T(4,128)S(1)} %get-tuple-element.11), channel_id=1, source_target_pairs={{4,0},{8,4},{12,8},{16,12},{20,16},{24,20},{28,24},{5,1},{9,5},{13... | collective-permute-start | bytes 36872 | tf_op jit(solution)/shard_map/ppermute | solution.py:22
  3.9 6.4 %collective-permute-start = (f32[3,16,64]{2,0,1:T(4,128)S(1)}, f32[3,16,64]{2,0,1:T(4,128)S(1)}, u32[]{:S(2)}, u32[]{:S(2)}) collective-permute-start(f32[3,16,64]{2,0,1:T(4,128)S(1)} %get-tuple-element.12), channel_id=1, source_target_pairs={{0,4},{4,8},{8,12},{12,16},{16,20},{20,24},{24,28},{1,5},{5,9},{9,... | collective-permute-start | bytes 36872 | tf_op jit(solution)/shard_map/ppermute | solution.py:22
  11.1 16.6 %collective-permute-start.2 = (f32[3,1,2176]{2,0,1:T(4,128)S(1)}, f32[3,1,2176]{2,0,1:T(4,128)S(1)}, u32[]{:S(2)}, u32[]{:S(2)}) collective-permute-start(f32[3,1,2176]{2,0,1:T(4,128)S(1)} %get-tuple-element.9), channel_id=1, source_target_pairs={{0,32},{32,64},{64,96},{96,128},{128,160},{160,192},{192,224},{224... | collective-permute-start | bytes 78344 | tf_op jit(solution)/shard_map/ppermute | solution.py:22
  15.3 12.3 %collective-permute-start.3 = (f32[3,1,2176]{2,0,1:T(4,128)S(1)}, f32[3,1,2176]{2,0,1:T(4,128)S(1)}, u32[]{:S(2)}, u32[]{:S(2)}) collective-permute-start(f32[3,1,2176]{2,0,1:T(4,128)S(1)} %get-tuple-element.10), channel_id=1, source_target_pairs={{32,0},{64,32},{96,64},{128,96},{160,128},{192,160},{224,192},{256... | collective-permute-start | bytes 78344 | tf_op jit(solution)/shard_map/ppermute | solution.py:22
  27.8 111.2 %copy-start = (f32[1,3,16,2048]{3,2,1,0:T(8,128)S(1)}, f32[1,3,16,2048]{3,2,1,0:T(8,128)}, u32[]{:S(2)}) copy-start(f32[1,3,16,2048]{3,2,1,0:T(8,128)} %param.4) | copy-start | bytes 1179652
  27.8 111.2 %copy-start.1 = (f32[1,3,16,2048]{3,2,1,0:T(8,128)S(1)}, f32[1,3,16,2048]{3,2,1,0:T(8,128)}, u32[]{:S(2)}) copy-start(f32[1,3,16,2048]{3,2,1,0:T(8,128)} %param.6) | copy-start | bytes 1179652
  27.9 111.2 %copy-start.2 = (f32[1,3,16,2048]{3,2,1,0:T(8,128)S(1)}, f32[1,3,16,2048]{3,2,1,0:T(8,128)}, u32[]{:S(2)}) copy-start(f32[1,3,16,2048]{3,2,1,0:T(8,128)} %param.5) | copy-start | bytes 1179652
  107.9 16.6 %collective-permute-start.5 = (f32[3,16,2048]{2,0,1:T(4,128)S(1)}, f32[3,16,2048]{2,0,1:T(4,128)S(1)}, u32[]{:S(2)}, u32[]{:S(2)}) collective-permute-start(f32[3,16,2048]{2,0,1:T(4,128)S(1)} %bitcast.23), channel_id=1, source_target_pairs={{0,1},{1,2},{2,3},{3,0},{4,5},{5,6},{6,7},{7,4},{8,9},{9,10},{10,1... | collective-permute-start | bytes 1179656 | tf_op jit(solution)/shard_map/ppermute | solution.py:27
  111.3 16.0 %collective-permute-start.6 = (f32[3,16,2048]{2,0,1:T(4,128)S(1)}, f32[3,16,2048]{2,0,1:T(4,128)S(1)}, u32[]{:S(2)}, u32[]{:S(2)}) collective-permute-start(f32[3,16,2048]{2,0,1:T(4,128)S(1)} %bitcast.24), channel_id=1, source_target_pairs={{0,3},{1,0},{2,1},{3,2},{4,7},{5,4},{6,5},{7,6},{8,11},{9,8},{10,9... | collective-permute-start | bytes 1179656 | tf_op jit(solution)/shard_map/ppermute | solution.py:27
  113.8 25.3 %collective-permute-start.4 = (f32[3,16,2048]{2,0,1:T(4,128)S(1)}, f32[3,16,2048]{2,0,1:T(4,128)S(1)}, u32[]{:S(2)}, u32[]{:S(2)}) collective-permute-start(f32[3,16,2048]{2,0,1:T(4,128)S(1)} %bitcast.25), channel_id=1, source_target_pairs={{0,2},{1,3},{2,0},{3,1},{4,6},{5,7},{6,4},{7,5},{8,10},{9,11},{10,... | collective-permute-start | bytes 1179656 | tf_op jit(solution)/shard_map/ppermute | solution.py:27

commit v2 on v1

--- a/solution.py
+++ b/solution.py
@@ -27,31 +27,33 @@
     return lax.ppermute(value, axis, [(source, (source + steps) % count) for source in range(count)])
 
 
-def force_kernel(rows, pairs, chunks, own_ref, halo_ref, flag_ref, out_ref, cbuf):
-    n_blocks = 2 * pairs + 1
+def force_kernel(rows, pairs, chunks, fresh, stride, own_ref, halo_ref, flag_ref, out_ref, cbuf):
+    n_blocks = 2 * chunks - 1
     left = lax.broadcasted_iota(jnp.int32, (ATOMS, LANES), 1) < ATOMS
 
     def build(h, slot):
         for c in range(3):
             prev = None
             for t in range(chunks):
-                if 2 * t - 1 >= n_blocks:
-                    break
                 r = halo_ref[h, c : c + 1, t * LANES : (t + 1) * LANES]
                 tt = jnp.transpose(jnp.broadcast_to(r, (LANES, LANES)))
-                if prev is not None and 2 * t - 1 < n_blocks:
+                if prev is not None:
                     cbuf[slot, c, 2 * t - 1] = jnp.where(left, prev[ATOMS:], tt[:ATOMS])
-                if 2 * t < n_blocks:
-                    cbuf[slot, c, 2 * t] = jnp.where(left, tt[:ATOMS], tt[ATOMS:])
+                cbuf[slot, c, 2 * t] = jnp.where(left, tt[:ATOMS], tt[ATOMS:])
                 prev = tt
 
-    build(0, 0)
-    build(1, 1)
+    if not fresh:
+        build(0, 0)
+        build(1, 1)
 
     offsets = ((0, 0),) + offsets_list
 
     def row_body(i, carry):
-        build(i + 2, lax.rem(i + 2, 3))
+        if fresh:
+            for j in range(3):
+                build(3 * i + j, j)
+        else:
+            build(i + 2, lax.rem(i + 2, 3))
 
         def pair_body(k, carry2):
             base = pl.multiple_of(k * LANES, LANES)
@@ -59,8 +61,8 @@
             flags = flag_ref[i, :, pl.ds(base, LANES)]
             acc = [jnp.zeros((8, LANES), jnp.float32) for _ in range(3)]
             for oi, (dx, dy) in enumerate(offsets):
-                slot = lax.rem(i + 1 + dx, 3)
-                n = 2 * k + 1 + dy
+                slot = dx + 1 if fresh else lax.rem(i + 1 + dx, 3)
+                n = stride * k + 1 + dy
                 if oi == 0:
                     f2 = jnp.full((8, LANES), 2.0, jnp.float32)
                     fh = jnp.full((8, LANES), 0.5, jnp.float32)
@@ -95,12 +97,12 @@
     lax.fori_loop(0, rows, row_body, 0)
 
 
-def cluster_forces(own, halo, flags):
+def cluster_forces(own, halo, flags, fresh=False, stride=2):
     rows, _, width = own.shape
     pairs = width // LANES
     chunks = halo.shape[2] // LANES
-    n_blocks = 2 * pairs + 1
-    kernel = lambda *refs: force_kernel(rows, pairs, chunks, *refs)
+    n_blocks = 2 * chunks - 1
+    kernel = lambda *refs: force_kernel(rows, pairs, chunks, fresh, stride, *refs)
     pair_count = rows * pairs * 9 * ATOMS * LANES
     return pl.pallas_call(
         kernel,
@@ -117,27 +119,72 @@
     )(own, halo, flags)
 
 
-def per_device(positions, velocities, noise, bonds):
-    rows_local = positions.shape[2]
-    cols_local = positions.shape[3] // ATOMS
-    width = cols_local * ATOMS
-    coords = positions[0]
-    lower_col = passed_along(coords[:, :, width - ATOMS :], "gy", 1)
-    upper_col = passed_along(coords[:, :, :ATOMS], "gy", -1)
-    widened = jnp.concatenate([lower_col, coords, upper_col], axis=2)
-    prev_row = passed_along(widened[:, rows_local - 1 :], "gx", 1)
-    next_row = passed_along(widened[:, :1], "gx", -1)
-    halo = jnp.concatenate([prev_row, widened, next_row], axis=1)
-    chunks = -(-(width + 2 * ATOMS) // LANES)
-    halo = jnp.pad(halo, ((0, 0), (0, 0), (0, chunks * LANES - width - 2 * ATOMS)))
-    halo = jnp.transpose(halo, (1, 0, 2))
-    own = jnp.transpose(coords, (1, 0, 2))
-    flags = jnp.repeat(jnp.transpose(bonds.astype(jnp.float32), (0, 2, 1)), ATOMS, axis=2)
-    force = jnp.transpose(cluster_forces(own, halo, flags), (1, 0, 2))
+def diagonal(value, steps_x, steps_y):
+    count_x, count_y = lax.axis_size("gx"), lax.axis_size("gy")
+    pairs = []
+    for source_x in range(count_x):
+        for source_y in range(count_y):
+            target_x, target_y = source_x + steps_x, source_y + steps_y
+            if 0 <= target_x < count_x and 0 <= target_y < count_y:
+                pairs.append((source_x * count_y + source_y, target_x * count_y + target_y))
+    return lax.ppermute(value, ("gx", "gy"), pairs)
+
+
+def replica_sum(force):
     across = ring_shift(force, "rep", 2)
     near = ring_shift(force, "rep", 1)
     far = ring_shift(force, "rep", 3)
-    summed_force = (force + across) + (near + far)
+    return (force + across) + (near + far)
+
+
+def per_device(positions, velocities, noise, bonds):
+    rows = positions.shape[2]
+    width = positions.shape[3]
+    coords = positions[0]
+    own = jnp.transpose(coords, (1, 0, 2))
+    flags = jnp.repeat(jnp.transpose(bonds.astype(jnp.float32), (0, 2, 1)), ATOMS, axis=2)
+    inner = cluster_forces(
+        own[1 : rows - 1, :, LANES : width - LANES],
+        own[:, :, ATOMS : width - ATOMS],
+        flags[1 : rows - 1, :, LANES : width - LANES],
+    )
+    lower_col = passed_along(coords[:, :, width - ATOMS :], "gy", 1)
+    upper_col = passed_along(coords[:, :, :ATOMS], "gy", -1)
+    prev_body = passed_along(coords[:, rows - 1 :], "gx", 1)
+    next_body = passed_along(coords[:, :1], "gx", -1)
+    prev_low = diagonal(coords[:, rows - 1 :, width - ATOMS :], 1, 1)
+    prev_high = diagonal(coords[:, rows - 1 :, :ATOMS], 1, -1)
+    next_low = diagonal(coords[:, :1, width - ATOMS :], -1, 1)
+    next_high = diagonal(coords[:, :1, :ATOMS], -1, -1)
+    pieces = (lower_col, upper_col, prev_body, next_body, prev_low, prev_high, next_low, next_high)
+    inner, pieces = lax.optimization_barrier((inner, pieces))
+    inner_sum = replica_sum(inner)
+    lower_col, upper_col, prev_body, next_body, prev_low, prev_high, next_low, next_high = pieces
+    widened = jnp.concatenate([lower_col, coords, upper_col], axis=2)
+    prev_row = jnp.concatenate([prev_low, prev_body, prev_high], axis=2)
+    next_row = jnp.concatenate([next_low, next_body, next_high], axis=2)
+    halo = jnp.transpose(jnp.concatenate([prev_row, widened, next_row], axis=1), (1, 0, 2))
+    edge_rows = cluster_forces(
+        jnp.concatenate([own[:1], own[rows - 1 :]], axis=0),
+        jnp.concatenate([halo[:3], halo[rows - 1 :]], axis=0),
+        jnp.concatenate([flags[:1], flags[rows - 1 :]], axis=0),
+        fresh=True,
+    )
+    edge_cols = cluster_forces(
+        jnp.concatenate([own[1 : rows - 1, :, :LANES], own[1 : rows - 1, :, width - LANES :]], axis=2),
+        jnp.concatenate([halo[1 : rows + 1, :, : 2 * LANES], halo[1 : rows + 1, :, width - 2 * LANES + 2 * ATOMS :]], axis=2),
+        jnp.concatenate([flags[1 : rows - 1, :, :LANES], flags[1 : rows - 1, :, width - LANES :]], axis=2),
+        stride=4,
+    )
+    edge_sum = replica_sum(
+        jnp.concatenate([edge_rows.reshape(-1, LANES), edge_cols.reshape(-1, LANES)], axis=0)
+    )
+    n_rows_part = edge_rows.size // LANES
+    rows_sum = edge_sum[:n_rows_part].reshape(edge_rows.shape)
+    cols_sum = edge_sum[n_rows_part:].reshape(edge_cols.shape)
+    middle = jnp.concatenate([cols_sum[:, :, :LANES], inner_sum, cols_sum[:, :, LANES:]], axis=2)
+    summed_force = jnp.concatenate([rows_sum[:1], middle, rows_sum[1:]], axis=0)
+    summed_force = jnp.transpose(summed_force, (1, 0, 2))
     mean_force = summed_force / lax.axis_size("rep")
     new_velocity = friction * velocities + time_step * mean_force[None] + noise_coef * noise
     new_position = positions + time_step * new_velocity

time: 144 us -> 169 us (1.17)
  the two profiles are of different devices: /device:TPU:26 before, /device:TPU:40 now
where the time goes in v2:
time: 169 us
  Pallas kernels  86 us (51%)
  starting transfers between devices  59.6 us (35%)
  waiting for transfers between devices  9.89 us (6%)
  local copies, waits for them, and re-layouts  9.59 us (6%)
  other arithmetic  2.52 us (1%)
    pallas_call x3, Pallas kernels, cluster_forces(): pl.pallas_call(kernel, out_shape=jax.ShapeDtypeStruct(own.shape, jnp.floa...  86 us
    ppermute x4, starting transfers between devices, diagonal(): return lax.ppermute(value, ('gx', 'gy'), pairs)  21.7 us
    ppermute x6, starting transfers between devices, ring_shift(): lax.ppermute(value, axis, [(source, (source + steps) % count) for source...  21.1 us
    ppermute x4, starting transfers between devices, passed_along(): lax.ppermute(value, axis, [(source, source + steps) for source in range(l...  16.8 us
    ppermute x6, waiting for transfers between devices, ring_shift(): lax.ppermute(value, axis, [(source, (source + steps) % count) for source...  9.87 us
    unnamed x13, local copies, waits for them, and re-layouts  4.23 us
  transfers between devices with their start and end apart: 14, of which 2 were waited for; matrix products, arithmetic and copies ran while one was open for 3% of the time, Pallas kernels for 37%

profile of v2, /device:TPU:40, one launch (start us, length us, event | category | flops | bytes accessed | tf_op | source)
XLA Modules:
  0.0 168.7 jit_solution(9552591327514064112)
XLA Ops:
  0.6 1.3 copy.32
  2.0 3.7 %collective-permute-start.4 = (f32[3,1,64]{2,0,1:T(4,128)S(1)}, f32[3,1,64]{2,0,1:T(4,128)S(1)}, u32[]{:S(2)}, u32[]{:S(2)}) collective-permute-start(f32[3,1,64]{2,0,1:T(4,128)S(1)} %get-tuple-element.40), channel_id=1, source_target_pairs={{0,36},{4,40},{8,44},{12,48},{16,52},{20,56},{24,60},{32,68},{36,7... | collective-permute-start | bytes 2312 | tf_op jit(solution)/shard_map/ppermute | solution.py:130
  5.7 7.6 %collective-permute-start.5 = (f32[3,1,64]{2,0,1:T(4,128)S(1)}, f32[3,1,64]{2,0,1:T(4,128)S(1)}, u32[]{:S(2)}, u32[]{:S(2)}) collective-permute-start(f32[3,1,64]{2,0,1:T(4,128)S(1)} %get-tuple-element.39), channel_id=1, source_target_pairs={{4,32},{8,36},{12,40},{16,44},{20,48},{24,52},{28,56},{36,64},{40,... | collective-permute-start | bytes 2312 | tf_op jit(solution)/shard_map/ppermute | solution.py:130
  13.3 3.7 %collective-permute-start.6 = (f32[3,1,64]{2,0,1:T(4,128)S(1)}, f32[3,1,64]{2,0,1:T(4,128)S(1)}, u32[]{:S(2)}, u32[]{:S(2)}) collective-permute-start(f32[3,1,64]{2,0,1:T(4,128)S(1)} %get-tuple-element.38), channel_id=1, source_target_pairs={{32,4},{36,8},{40,12},{44,16},{48,20},{52,24},{56,28},{64,36},{68,... | collective-permute-start | bytes 2312 | tf_op jit(solution)/shard_map/ppermute | solution.py:130
  17.0 6.7 %collective-permute-start.7 = (f32[3,1,64]{2,0,1:T(4,128)S(1)}, f32[3,1,64]{2,0,1:T(4,128)S(1)}, u32[]{:S(2)}, u32[]{:S(2)}) collective-permute-start(f32[3,1,64]{2,0,1:T(4,128)S(1)} %get-tuple-element.37), channel_id=1, source_target_pairs={{36,0},{40,4},{44,8},{48,12},{52,16},{56,20},{60,24},{68,32},{72,3... | collective-permute-start | bytes 2312 | tf_op jit(solution)/shard_map/ppermute | solution.py:130
  23.7 1.9 %collective-permute-start = (f32[3,16,64]{2,0,1:T(4,128)S(1)}, f32[3,16,64]{2,0,1:T(4,128)S(1)}, u32[]{:S(2)}, u32[]{:S(2)}) collective-permute-start(f32[3,16,64]{2,0,1:T(4,128)S(1)} %get-tuple-element.44), channel_id=1, source_target_pairs={{0,4},{4,8},{8,12},{12,16},{16,20},{20,24},{24,28},{1,5},{5,9},{9,... | collective-permute-start | bytes 36872 | tf_op jit(solution)/shard_map/ppermute | solution.py:22
  25.7 0.8 convert_bitcast_fusion
  26.6 0.6 broadcast_in_dim.12
  27.2 1.6 reshape.32
  28.8 0.9 fusion.2
  30.3 0.3 slice.136.refs_1_
  30.7 5.8 %collective-permute-start.1 = (f32[3,16,64]{2,0,1:T(4,128)S(1)}, f32[3,16,64]{2,0,1:T(4,128)S(1)}, u32[]{:S(2)}, u32[]{:S(2)}) collective-permute-start(f32[3,16,64]{2,0,1:T(4,128)S(1)} %get-tuple-element.43), channel_id=1, source_target_pairs={{4,0},{8,4},{12,8},{16,12},{20,16},{24,20},{28,24},{5,1},{9,5},{13... | collective-permute-start | bytes 36872 | tf_op jit(solution)/shard_map/ppermute | solution.py:22
  36.5 1.9 %collective-permute-start.2 = (f32[3,1,2048]{2,0,1:T(4,128)S(1)}, f32[3,1,2048]{2,0,1:T(4,128)S(1)}, u32[]{:S(2)}, u32[]{:S(2)}) collective-permute-start(f32[3,1,2048]{2,0,1:T(4,128)S(1)} %get-tuple-element.42), channel_id=1, source_target_pairs={{0,32},{32,64},{64,96},{96,128},{128,160},{160,192},{192,224},{224... | collective-permute-start | bytes 73736 | tf_op jit(solution)/shard_map/ppermute | solution.py:22
  38.4 7.2 %collective-permute-start.3 = (f32[3,1,2048]{2,0,1:T(4,128)S(1)}, f32[3,1,2048]{2,0,1:T(4,128)S(1)}, u32[]{:S(2)}, u32[]{:S(2)}) collective-permute-start(f32[3,1,2048]{2,0,1:T(4,128)S(1)} %get-tuple-element.41), channel_id=1, source_target_pairs={{32,0},{64,32},{96,64},{128,96},{160,128},{192,160},{224,192},{256... | collective-permute-start | bytes 73736 | tf_op jit(solution)/shard_map/ppermute | solution.py:22
  45.7 61.7 %shard_map.67 = f32[14,3,1792]{2,1,0:T(4,128)S(1)} custom-call(f32[14,3,1792]{2,1,0:T(4,128)S(1)} %slice.135.refs_0_, f32[16,3,1920]{2,1,0:T(4,128)S(1)} %slice.136.refs_1_, f32[14,8,1792]{2,1,0:T(8,128)S(1)} %slice.137.refs_2_), custom_call_target="tpu_custom_call" | custom-call | flops 289013760 | bytes 1773568 | tf_op jit(solution)/shard_map/pallas_call | solution.py:107
  107.5 0.7 concatenate.41
  108.7 11.2 %shard_map.69 = f32[14,3,256]{2,1,0:T(4,128)S(1)} custom-call(f32[14,3,256]{2,1,0:T(4,128)S(1)} %pad_maximum_fusion.6.refs_0_, f32[16,3,512]{2,1,0:T(4,128)S(1)} %pad_maximum_fusion.3.refs_1_, f32[14,8,256]{2,1,0:T(8,128)S(1)} %pad_maximum_fusion.4.refs_2_), custom_call_target="tpu_custom_call" | custom-call | flops 41287680 | bytes 299008 | tf_op jit(solution)/shard_map/pallas_call | solution.py:107
  119.9 13.1 %shard_map.68 = f32[2,3,2048]{2,1,0:T(4,128)S(1)} custom-call(f32[2,3,2048]{2,1,0:T(4,128)S(1)} %pad_maximum_fusion.5.refs_0_, f32[6,3,2176]{2,1,0:T(4,128)S(1)} %pad_maximum_fusion.1.refs_1_, f32[2,8,2048]{2,1,0:T(8,128)S(1)} %pad_maximum_fusion.2.refs_2_), custom_call_target="tpu_custom_call" | custom-call | flops 47185920 | bytes 386048 | tf_op jit(solution)/shard_map/pallas_call | solution.py:107
  133.2 4.8 %collective-permute-start.10 = (f32[180,128]{1,0:T(8,128)S(1)}, f32[180,128]{1,0:T(8,128)S(1)}, u32[]{:S(2)}, u32[]{:S(2)}) collective-permute-start(f32[180,128]{1,0:T(8,128)S(1)} %constant_dynamic-update-slice_fusion), channel_id=1, source_target_pairs={{0,3},{1,0},{2,1},{3,2},{4,7},{5,4},{6,5},{7,6},{8,11},{9,8},{10,9... | collective-permute-start | bytes 276488 | tf_op jit(solution)/shard_map/ppermute | solution.py:27
  138.0 2.7 %collective-permute-start.8 = (f32[180,128]{1,0:T(8,128)S(1)}, f32[180,128]{1,0:T(8,128)S(1)}, u32[]{:S(2)}, u32[]{:S(2)}) collective-permute-start(f32[180,128]{1,0:T(8,128)S(1)} %constant_dynamic-update-slice_fusion), channel_id=1, source_target_pairs={{0,2},{1,3},{2,0},{3,1},{4,6},{5,7},{6,4},{7,5},{8,10},{9,11},{10,... | collective-permute-start | bytes 276488 | tf_op jit(solution)/shard_map/ppermute | solution.py:27
  140.7 2.8 %collective-permute-start.9 = (f32[180,128]{1,0:T(8,128)S(1)}, f32[180,128]{1,0:T(8,128)S(1)}, u32[]{:S(2)}, u32[]{:S(2)}) collective-permute-start(f32[180,128]{1,0:T(8,128)S(1)} %constant_dynamic-update-slice_fusion), channel_id=1, source_target_pairs={{0,1},{1,2},{2,3},{3,0},{4,5},{5,6},{6,7},{7,4},{8,9},{9,10},{10,1... | collective-permute-start | bytes 276488 | tf_op jit(solution)/shard_map/ppermute | solution.py:27
  143.5 3.8 %collective-permute-start.11 = (f32[14,3,1792]{2,1,0:T(4,128)S(1)}, f32[14,3,1792]{2,1,0:T(4,128)S(1)}, u32[]{:S(2)}, u32[]{:S(2)}) collective-permute-start(f32[14,3,1792]{2,1,0:T(4,128)S(1)} %shard_map.67), channel_id=1, source_target_pairs={{0,2},{1,3},{2,0},{3,1},{4,6},{5,7},{6,4},{7,5},{8,10},{9,11},{10,... | collective-permute-start | bytes 903176 | tf_op jit(solution)/shard_map/ppermute | solution.py:27
  147.3 3.3 %collective-permute-start.12 = (f32[14,3,1792]{2,1,0:T(4,128)S(1)}, f32[14,3,1792]{2,1,0:T(4,128)S(1)}, u32[]{:S(2)}, u32[]{:S(2)}) collective-permute-start(f32[14,3,1792]{2,1,0:T(4,128)S(1)} %shard_map.67), channel_id=1, source_target_pairs={{0,1},{1,2},{2,3},{3,0},{4,5},{5,6},{6,7},{7,4},{8,9},{9,10},{10,1... | collective-permute-start | bytes 903176 | tf_op jit(solution)/shard_map/ppermute | solution.py:27
  150.5 3.8 %collective-permute-start.13 = (f32[14,3,1792]{2,1,0:T(4,128)S(1)}, f32[14,3,1792]{2,1,0:T(4,128)S(1)}, u32[]{:S(2)}, u32[]{:S(2)}) collective-permute-start(f32[14,3,1792]{2,1,0:T(4,128)S(1)} %shard_map.67), channel_id=1, source_target_pairs={{0,3},{1,0},{2,1},{3,2},{4,7},{5,4},{6,5},{7,6},{8,11},{9,8},{10,9... | collective-permute-start | bytes 903176 | tf_op jit(solution)/shard_map/ppermute | solution.py:27
  154.5 4.6 %collective-permute-done.11 = f32[14,3,1792]{2,1,0:T(4,128)S(1)} collective-permute-done((f32[14,3,1792]{2,1,0:T(4,128)S(1)}, f32[14,3,1792]{2,1,0:T(4,128)S(1)}, u32[]{:S(2)}, u32[]{:S(2)}) %collective-permute-start.11) | collective-permute-done | bytes 301088 | tf_op jit(solution)/shard_map/ppermute | solution.py:27
  159.1 5.2 %collective-permute-done.12 = f32[14,3,1792]{2,1,0:T(4,128)S(1)} collective-permute-done((f32[14,3,1792]{2,1,0:T(4,128)S(1)}, f32[14,3,1792]{2,1,0:T(4,128)S(1)}, u32[]{:S(2)}, u32[]{:S(2)}) %collective-permute-start.12) | collective-permute-done | bytes 301088 | tf_op jit(solution)/shard_map/ppermute | solution.py:27
  164.4 0.2 add_add_fusion
  164.5 0.1 multiply_bitcast_fusion
  164.7 1.0 copy_add_fusion
  165.8 1.0 copy.19
  166.8 1.0 copy.20
  167.7 1.0 copy.18
  (54 shorter events, 1.5 us)
Async XLA Ops:
  2.0 28.8 %collective-permute-start.4 = (f32[3,1,64]{2,0,1:T(4,128)S(1)}, f32[3,1,64]{2,0,1:T(4,128)S(1)}, u32[]{:S(2)}, u32[]{:S(2)}) collective-permute-start(f32[3,1,64]{2,0,1:T(4,128)S(1)} %get-tuple-element.40), channel_id=1, source_target_pairs={{0,36},{4,40},{8,44},{12,48},{16,52},{20,56},{24,60},{32,68},{36,7... | collective-permute-start | bytes 2312 | tf_op jit(solution)/shard_map/ppermute | solution.py:130
  5.7 30.8 %collective-permute-start.5 = (f32[3,1,64]{2,0,1:T(4,128)S(1)}, f32[3,1,64]{2,0,1:T(4,128)S(1)}, u32[]{:S(2)}, u32[]{:S(2)}) collective-permute-start(f32[3,1,64]{2,0,1:T(4,128)S(1)} %get-tuple-element.39), channel_id=1, source_target_pairs={{4,32},{8,36},{12,40},{16,44},{20,48},{24,52},{28,56},{36,64},{40,... | collective-permute-start | bytes 2312 | tf_op jit(solution)/shard_map/ppermute | solution.py:130
  13.3 25.2 %collective-permute-start.6 = (f32[3,1,64]{2,0,1:T(4,128)S(1)}, f32[3,1,64]{2,0,1:T(4,128)S(1)}, u32[]{:S(2)}, u32[]{:S(2)}) collective-permute-start(f32[3,1,64]{2,0,1:T(4,128)S(1)} %get-tuple-element.38), channel_id=1, source_target_pairs={{32,4},{36,8},{40,12},{44,16},{48,20},{52,24},{56,28},{64,36},{68,... | collective-permute-start | bytes 2312 | tf_op jit(solution)/shard_map/ppermute | solution.py:130
  17.0 90.4 %collective-permute-start.7 = (f32[3,1,64]{2,0,1:T(4,128)S(1)}, f32[3,1,64]{2,0,1:T(4,128)S(1)}, u32[]{:S(2)}, u32[]{:S(2)}) collective-permute-start(f32[3,1,64]{2,0,1:T(4,128)S(1)} %get-tuple-element.37), channel_id=1, source_target_pairs={{36,0},{40,4},{44,8},{48,12},{52,16},{56,20},{60,24},{68,32},{72,3... | collective-permute-start | bytes 2312 | tf_op jit(solution)/shard_map/ppermute | solution.py:130
  23.7 83.7 %collective-permute-start = (f32[3,16,64]{2,0,1:T(4,128)S(1)}, f32[3,16,64]{2,0,1:T(4,128)S(1)}, u32[]{:S(2)}, u32[]{:S(2)}) collective-permute-start(f32[3,16,64]{2,0,1:T(4,128)S(1)} %get-tuple-element.44), channel_id=1, source_target_pairs={{0,4},{4,8},{8,12},{12,16},{16,20},{20,24},{24,28},{1,5},{5,9},{9,... | collective-permute-start | bytes 36872 | tf_op jit(solution)/shard_map/ppermute | solution.py:22
  28.8 1.8 %copy-start = (f32[16,8,2048]{2,1,0:T(8,128)S(1)}, f32[16,8,2048]{2,1,0:T(8,128)}, u32[]{:S(2)}) copy-start(f32[16,8,2048]{2,1,0:T(8,128)} %reshape.32) | copy-start | bytes 3145732
  30.7 76.7 %collective-permute-start.1 = (f32[3,16,64]{2,0,1:T(4,128)S(1)}, f32[3,16,64]{2,0,1:T(4,128)S(1)}, u32[]{:S(2)}, u32[]{:S(2)}) collective-permute-start(f32[3,16,64]{2,0,1:T(4,128)S(1)} %get-tuple-element.43), channel_id=1, source_target_pairs={{4,0},{8,4},{12,8},{16,12},{20,16},{24,20},{28,24},{5,1},{9,5},{13... | collective-permute-start | bytes 36872 | tf_op jit(solution)/shard_map/ppermute | solution.py:22
  36.5 70.9 %collective-permute-start.2 = (f32[3,1,2048]{2,0,1:T(4,128)S(1)}, f32[3,1,2048]{2,0,1:T(4,128)S(1)}, u32[]{:S(2)}, u32[]{:S(2)}) collective-permute-start(f32[3,1,2048]{2,0,1:T(4,128)S(1)} %get-tuple-element.42), channel_id=1, source_target_pairs={{0,32},{32,64},{64,96},{96,128},{128,160},{160,192},{192,224},{224... | collective-permute-start | bytes 73736 | tf_op jit(solution)/shard_map/ppermute | solution.py:22
  38.4 69.0 %collective-permute-start.3 = (f32[3,1,2048]{2,0,1:T(4,128)S(1)}, f32[3,1,2048]{2,0,1:T(4,128)S(1)}, u32[]{:S(2)}, u32[]{:S(2)}) collective-permute-start(f32[3,1,2048]{2,0,1:T(4,128)S(1)} %get-tuple-element.41), channel_id=1, source_target_pairs={{32,0},{64,32},{96,64},{128,96},{160,128},{192,160},{224,192},{256... | collective-permute-start | bytes 73736 | tf_op jit(solution)/shard_map/ppermute | solution.py:22
  133.1 31.6 %copy-start.1 = (f32[1,3,16,2048]{3,2,1,0:T(8,128)S(1)}, f32[1,3,16,2048]{3,2,1,0:T(8,128)}, u32[]{:S(2)}) copy-start(f32[1,3,16,2048]{3,2,1,0:T(8,128)} %param.4) | copy-start | bytes 1179652
  133.1 31.6 %copy-start.2 = (f32[1,3,16,2048]{3,2,1,0:T(8,128)S(1)}, f32[1,3,16,2048]{3,2,1,0:T(8,128)}, u32[]{:S(2)}) copy-start(f32[1,3,16,2048]{3,2,1,0:T(8,128)} %param.6) | copy-start | bytes 1179652
  133.1 31.6 %copy-start.3 = (f32[1,3,16,2048]{3,2,1,0:T(8,128)S(1)}, f32[1,3,16,2048]{3,2,1,0:T(8,128)}, u32[]{:S(2)}) copy-start(f32[1,3,16,2048]{3,2,1,0:T(8,128)} %param.5) | copy-start | bytes 1179652
  133.2 17.4 %collective-permute-start.10 = (f32[180,128]{1,0:T(8,128)S(1)}, f32[180,128]{1,0:T(8,128)S(1)}, u32[]{:S(2)}, u32[]{:S(2)}) collective-permute-start(f32[180,128]{1,0:T(8,128)S(1)} %constant_dynamic-update-slice_fusion), channel_id=1, source_target_pairs={{0,3},{1,0},{2,1},{3,2},{4,7},{5,4},{6,5},{7,6},{8,11},{9,8},{10,9... | collective-permute-start | bytes 276488 | tf_op jit(solution)/shard_map/ppermute | solution.py:27
  138.0 16.4 %collective-permute-start.8 = (f32[180,128]{1,0:T(8,128)S(1)}, f32[180,128]{1,0:T(8,128)S(1)}, u32[]{:S(2)}, u32[]{:S(2)}) collective-permute-start(f32[180,128]{1,0:T(8,128)S(1)} %constant_dynamic-update-slice_fusion), channel_id=1, source_target_pairs={{0,2},{1,3},{2,0},{3,1},{4,6},{5,7},{6,4},{7,5},{8,10},{9,11},{10,... | collective-permute-start | bytes 276488 | tf_op jit(solution)/shard_map/ppermute | solution.py:27
  140.7 13.7 %collective-permute-start.9 = (f32[180,128]{1,0:T(8,128)S(1)}, f32[180,128]{1,0:T(8,128)S(1)}, u32[]{:S(2)}, u32[]{:S(2)}) collective-permute-start(f32[180,128]{1,0:T(8,128)S(1)} %constant_dynamic-update-slice_fusion), channel_id=1, source_target_pairs={{0,1},{1,2},{2,3},{3,0},{4,5},{5,6},{6,7},{7,4},{8,9},{9,10},{10,1... | collective-permute-start | bytes 276488 | tf_op jit(solution)/shard_map/ppermute | solution.py:27
  143.5 15.6 %collective-permute-start.11 = (f32[14,3,1792]{2,1,0:T(4,128)S(1)}, f32[14,3,1792]{2,1,0:T(4,128)S(1)}, u32[]{:S(2)}, u32[]{:S(2)}) collective-permute-start(f32[14,3,1792]{2,1,0:T(4,128)S(1)} %shard_map.67), channel_id=1, source_target_pairs={{0,2},{1,3},{2,0},{3,1},{4,6},{5,7},{6,4},{7,5},{8,10},{9,11},{10,... | collective-permute-start | bytes 903176 | tf_op jit(solution)/shard_map/ppermute | solution.py:27
  147.3 17.1 %collective-permute-start.12 = (f32[14,3,1792]{2,1,0:T(4,128)S(1)}, f32[14,3,1792]{2,1,0:T(4,128)S(1)}, u32[]{:S(2)}, u32[]{:S(2)}) collective-permute-start(f32[14,3,1792]{2,1,0:T(4,128)S(1)} %shard_map.67), channel_id=1, source_target_pairs={{0,1},{1,2},{2,3},{3,0},{4,5},{5,6},{6,7},{7,4},{8,9},{9,10},{10,1... | collective-permute-start | bytes 903176 | tf_op jit(solution)/shard_map/ppermute | solution.py:27
  150.5 13.8 %collective-permute-start.13 = (f32[14,3,1792]{2,1,0:T(4,128)S(1)}, f32[14,3,1792]{2,1,0:T(4,128)S(1)}, u32[]{:S(2)}, u32[]{:S(2)}) collective-permute-start(f32[14,3,1792]{2,1,0:T(4,128)S(1)} %shard_map.67), channel_id=1, source_target_pairs={{0,3},{1,0},{2,1},{3,2},{4,7},{5,4},{6,5},{7,6},{8,11},{9,8},{10,9... | collective-permute-start | bytes 903176 | tf_op jit(solution)/shard_map/ppermute | solution.py:27

commit v3 on v1

--- a/solution.py
+++ b/solution.py
@@ -134,10 +134,8 @@
     own = jnp.transpose(coords, (1, 0, 2))
     flags = jnp.repeat(jnp.transpose(bonds.astype(jnp.float32), (0, 2, 1)), ATOMS, axis=2)
     force = jnp.transpose(cluster_forces(own, halo, flags), (1, 0, 2))
-    across = ring_shift(force, "rep", 2)
-    near = ring_shift(force, "rep", 1)
-    far = ring_shift(force, "rep", 3)
-    summed_force = (force + across) + (near + far)
+    paired = force + ring_shift(force, "rep", 2)
+    summed_force = paired + ring_shift(paired, "rep", 1)
     mean_force = summed_force / lax.axis_size("rep")
     new_velocity = friction * velocities + time_step * mean_force[None] + noise_coef * noise
     new_position = positions + time_step * new_velocity

time: 144 us -> 147 us (1.021)
  the two profiles are of different devices: /device:TPU:26 before, /device:TPU:24 now
where the time goes in v3:
time: 147 us
  Pallas kernels  80 us (54%)
  waiting for transfers between devices  29.6 us (20%)
  starting transfers between devices  25.6 us (17%)
  local copies, waits for them, and re-layouts  9.09 us (6%)
  other arithmetic  1.57 us (1%)
    pallas_call x1, Pallas kernels, cluster_forces(): pl.pallas_call(kernel, out_shape=jax.ShapeDtypeStruct(own.shape, jnp.floa...  80 us
    ppermute x2, waiting for transfers between devices, ring_shift(): lax.ppermute(value, axis, [(source, (source + steps) % count) for source...  25.9 us
    ppermute x4, starting transfers between devices, passed_along(): lax.ppermute(value, axis, [(source, source + steps) for source in range(l...  17.1 us
    ppermute x2, starting transfers between devices, ring_shift(): lax.ppermute(value, axis, [(source, (source + steps) % count) for source...  8.46 us
    unnamed x12, local copies, waits for them, and re-layouts  4.26 us
    ppermute x4, waiting for transfers between devices, passed_along(): lax.ppermute(value, axis, [(source, source + steps) for source in range(l...  3.72 us
  transfers between devices with their start and end apart: 6, of which 3 were waited for; matrix products, arithmetic and copies ran while one was open for 3% of the time, Pallas kernels for 0%

profile of v3, /device:TPU:24, one launch (start us, length us, event | category | flops | bytes accessed | tf_op | source)
XLA Modules:
  0.0 146.7 jit_solution(10382145393341460432)
XLA Ops:
  0.6 0.0 copy-start.3
  0.6 1.3 copy.25
  1.9 0.1 fusion.3
  2.0 1.9 %collective-permute-start.1 = (f32[3,16,64]{2,0,1:T(4,128)S(1)}, f32[3,16,64]{2,0,1:T(4,128)S(1)}, u32[]{:S(2)}, u32[]{:S(2)}) collective-permute-start(f32[3,16,64]{2,0,1:T(4,128)S(1)} %get-tuple-element.10), channel_id=1, source_target_pairs={{4,0},{8,4},{12,8},{16,12},{20,16},{24,20},{28,24},{5,1},{9,5},{13... | collective-permute-start | bytes 36872 | tf_op jit(solution)/shard_map/ppermute | solution.py:22
  3.9 2.4 %collective-permute-start = (f32[3,16,64]{2,0,1:T(4,128)S(1)}, f32[3,16,64]{2,0,1:T(4,128)S(1)}, u32[]{:S(2)}, u32[]{:S(2)}) collective-permute-start(f32[3,16,64]{2,0,1:T(4,128)S(1)} %get-tuple-element.11), channel_id=1, source_target_pairs={{0,4},{4,8},{8,12},{12,16},{16,20},{20,24},{24,28},{1,5},{5,9},{9,... | collective-permute-start | bytes 36872 | tf_op jit(solution)/shard_map/ppermute | solution.py:22
  6.4 0.0 collective-permute-done.1
  6.4 3.7 %collective-permute-done = f32[3,16,64]{2,0,1:T(4,128)S(1)} collective-permute-done((f32[3,16,64]{2,0,1:T(4,128)S(1)}, f32[3,16,64]{2,0,1:T(4,128)S(1)}, u32[]{:S(2)}, u32[]{:S(2)}) %collective-permute-start) | collective-permute-done | bytes 12320 | tf_op jit(solution)/shard_map/ppermute | solution.py:22
  10.1 0.7 concatenate.6
  10.8 4.5 %collective-permute-start.2 = (f32[3,1,2176]{2,0,1:T(4,128)S(1)}, f32[3,1,2176]{2,0,1:T(4,128)S(1)}, u32[]{:S(2)}, u32[]{:S(2)}) collective-permute-start(f32[3,1,2176]{2,0,1:T(4,128)S(1)} %get-tuple-element.8), channel_id=1, source_target_pairs={{0,32},{32,64},{64,96},{96,128},{128,160},{160,192},{192,224},{224... | collective-permute-start | bytes 78344 | tf_op jit(solution)/shard_map/ppermute | solution.py:22
  15.3 8.3 %collective-permute-start.3 = (f32[3,1,2176]{2,0,1:T(4,128)S(1)}, f32[3,1,2176]{2,0,1:T(4,128)S(1)}, u32[]{:S(2)}, u32[]{:S(2)}) collective-permute-start(f32[3,1,2176]{2,0,1:T(4,128)S(1)} %get-tuple-element.9), channel_id=1, source_target_pairs={{32,0},{64,32},{96,64},{128,96},{160,128},{192,160},{224,192},{256... | collective-permute-start | bytes 78344 | tf_op jit(solution)/shard_map/ppermute | solution.py:22
  23.6 0.0 copy-done.3
  23.6 1.9 %broadcast_in_dim.4 = f32[16,8,32,64]{3,2,1,0:T(8,128)} broadcast(f32[16,8,32]{2,1,0:T(8,128)S(1)} %convert_bitcast_fusion), dimensions={0,1,2} | broadcast | bytes 1064960 | tf_op jit(solution)/shard_map/broadcast_in_dim | solution.py:135
  25.6 2.1 %reshape.10.refs_2_ = f32[16,8,2048]{2,1,0:T(8,128)S(1)} reshape(f32[16,8,32,64]{3,2,1,0:T(8,128)} %broadcast_in_dim.4) | data formatting | bytes 2097152 | tf_op jit(solution)/shard_map/reshape | solution.py:135
  27.7 0.0 collective-permute-done.2
  27.7 0.0 collective-permute-done.3
  27.7 0.1 maximum_bitcast_fusion.refs_1_
  27.8 80.0 %shard_map.67 = f32[16,3,2048]{2,1,0:T(4,128)S(1)} custom-call(f32[16,3,2048]{2,1,0:T(4,128)S(1)} %bitcast.21, f32[18,3,2176]{2,1,0:T(4,128)S(1)} %maximum_bitcast_fusion.refs_1_, f32[16,8,2048]{2,1,0:T(8,128)S(1)} %reshape.10.refs_2_), custom_call_target="tpu_custom_call" | custom-call | flops 377487360 | bytes 2305024 | tf_op jit(solution)/shard_map/pallas_call | solution.py:105
  107.9 0.0 copy-start
  107.9 0.0 copy-start.1
  107.9 0.0 copy-start.2
  107.9 5.1 %collective-permute-start.4 = (f32[3,16,2048]{2,0,1:T(4,128)S(1)}, f32[3,16,2048]{2,0,1:T(4,128)S(1)}, u32[]{:S(2)}, u32[]{:S(2)}) collective-permute-start(f32[3,16,2048]{2,0,1:T(4,128)S(1)} %bitcast.22), channel_id=1, source_target_pairs={{0,2},{1,3},{2,0},{3,1},{4,6},{5,7},{6,4},{7,5},{8,10},{9,11},{10,... | collective-permute-start | bytes 1179656 | tf_op jit(solution)/shard_map/ppermute | solution.py:27
  113.0 12.7 %collective-permute-done.4 = f32[3,16,2048]{2,0,1:T(4,128)S(1)} collective-permute-done((f32[3,16,2048]{2,0,1:T(4,128)S(1)}, f32[3,16,2048]{2,0,1:T(4,128)S(1)}, u32[]{:S(2)}, u32[]{:S(2)}) %collective-permute-start.4) | collective-permute-done | bytes 393248 | tf_op jit(solution)/shard_map/ppermute | solution.py:27
  125.7 0.2 bitcast_add_fusion.1
  125.9 3.4 %collective-permute-start.5 = (f32[3,16,2048]{2,0,1:T(4,128)S(1)}, f32[3,16,2048]{2,0,1:T(4,128)S(1)}, u32[]{:S(2)}, u32[]{:S(2)}) collective-permute-start(f32[3,16,2048]{2,0,1:T(4,128)S(1)} %bitcast_add_fusion.1), channel_id=1, source_target_pairs={{0,1},{1,2},{2,3},{3,0},{4,5},{5,6},{6,7},{7,4},{8,9},{9,10},{10,1... | collective-permute-start | bytes 1179656 | tf_op jit(solution)/shard_map/ppermute | solution.py:27
  129.3 13.2 %collective-permute-done.5 = f32[3,16,2048]{2,0,1:T(4,128)S(1)} collective-permute-done((f32[3,16,2048]{2,0,1:T(4,128)S(1)}, f32[3,16,2048]{2,0,1:T(4,128)S(1)}, u32[]{:S(2)}, u32[]{:S(2)}) %collective-permute-start.5) | collective-permute-done | bytes 393248 | tf_op jit(solution)/shard_map/ppermute | solution.py:27
  142.4 0.2 broadcast_multiply_fusion
  142.6 1.0 copy.11
  143.6 0.0 copy-done
  143.6 0.0 copy-done.1
  143.6 1.1 copy_add_fusion
  144.7 1.0 copy.13
  145.7 1.0 copy.12
  (3 shorter events, 0.0 us)
Async XLA Ops:
  0.6 23.0 %copy-start.3 = (s32[16,32,8]{1,2,0:T(8,128)S(1)}, s32[16,32,8]{1,2,0:T(8,128)}, u32[]{:S(2)}) copy-start(s32[16,32,8]{1,2,0:T(8,128)} %param.7) | copy-start | bytes 49156
  2.0 4.3 %collective-permute-start.1 = (f32[3,16,64]{2,0,1:T(4,128)S(1)}, f32[3,16,64]{2,0,1:T(4,128)S(1)}, u32[]{:S(2)}, u32[]{:S(2)}) collective-permute-start(f32[3,16,64]{2,0,1:T(4,128)S(1)} %get-tuple-element.10), channel_id=1, source_target_pairs={{4,0},{8,4},{12,8},{16,12},{20,16},{24,20},{28,24},{5,1},{9,5},{13... | collective-permute-start | bytes 36872 | tf_op jit(solution)/shard_map/ppermute | solution.py:22
  3.9 6.1 %collective-permute-start = (f32[3,16,64]{2,0,1:T(4,128)S(1)}, f32[3,16,64]{2,0,1:T(4,128)S(1)}, u32[]{:S(2)}, u32[]{:S(2)}) collective-permute-start(f32[3,16,64]{2,0,1:T(4,128)S(1)} %get-tuple-element.11), channel_id=1, source_target_pairs={{0,4},{4,8},{8,12},{12,16},{16,20},{20,24},{24,28},{1,5},{5,9},{9,... | collective-permute-start | bytes 36872 | tf_op jit(solution)/shard_map/ppermute | solution.py:22
  10.8 16.8 %collective-permute-start.2 = (f32[3,1,2176]{2,0,1:T(4,128)S(1)}, f32[3,1,2176]{2,0,1:T(4,128)S(1)}, u32[]{:S(2)}, u32[]{:S(2)}) collective-permute-start(f32[3,1,2176]{2,0,1:T(4,128)S(1)} %get-tuple-element.8), channel_id=1, source_target_pairs={{0,32},{32,64},{64,96},{96,128},{128,160},{160,192},{192,224},{224... | collective-permute-start | bytes 78344 | tf_op jit(solution)/shard_map/ppermute | solution.py:22
  15.3 12.3 %collective-permute-start.3 = (f32[3,1,2176]{2,0,1:T(4,128)S(1)}, f32[3,1,2176]{2,0,1:T(4,128)S(1)}, u32[]{:S(2)}, u32[]{:S(2)}) collective-permute-start(f32[3,1,2176]{2,0,1:T(4,128)S(1)} %get-tuple-element.9), channel_id=1, source_target_pairs={{32,0},{64,32},{96,64},{128,96},{160,128},{192,160},{224,192},{256... | collective-permute-start | bytes 78344 | tf_op jit(solution)/shard_map/ppermute | solution.py:22
  107.9 35.7 %copy-start = (f32[1,3,16,2048]{3,2,1,0:T(8,128)S(1)}, f32[1,3,16,2048]{3,2,1,0:T(8,128)}, u32[]{:S(2)}) copy-start(f32[1,3,16,2048]{3,2,1,0:T(8,128)} %param.4) | copy-start | bytes 1179652
  107.9 35.7 %copy-start.1 = (f32[1,3,16,2048]{3,2,1,0:T(8,128)S(1)}, f32[1,3,16,2048]{3,2,1,0:T(8,128)}, u32[]{:S(2)}) copy-start(f32[1,3,16,2048]{3,2,1,0:T(8,128)} %param.6) | copy-start | bytes 1179652
  107.9 35.7 %copy-start.2 = (f32[1,3,16,2048]{3,2,1,0:T(8,128)S(1)}, f32[1,3,16,2048]{3,2,1,0:T(8,128)}, u32[]{:S(2)}) copy-start(f32[1,3,16,2048]{3,2,1,0:T(8,128)} %param.5) | copy-start | bytes 1179652
  107.9 17.8 %collective-permute-start.4 = (f32[3,16,2048]{2,0,1:T(4,128)S(1)}, f32[3,16,2048]{2,0,1:T(4,128)S(1)}, u32[]{:S(2)}, u32[]{:S(2)}) collective-permute-start(f32[3,16,2048]{2,0,1:T(4,128)S(1)} %bitcast.22), channel_id=1, source_target_pairs={{0,2},{1,3},{2,0},{3,1},{4,6},{5,7},{6,4},{7,5},{8,10},{9,11},{10,... | collective-permute-start | bytes 1179656 | tf_op jit(solution)/shard_map/ppermute | solution.py:27
  125.9 16.6 %collective-permute-start.5 = (f32[3,16,2048]{2,0,1:T(4,128)S(1)}, f32[3,16,2048]{2,0,1:T(4,128)S(1)}, u32[]{:S(2)}, u32[]{:S(2)}) collective-permute-start(f32[3,16,2048]{2,0,1:T(4,128)S(1)} %bitcast_add_fusion.1), channel_id=1, source_target_pairs={{0,1},{1,2},{2,3},{3,0},{4,5},{5,6},{6,7},{7,4},{8,9},{9,10},{10,1... | collective-permute-start | bytes 1179656 | tf_op jit(solution)/shard_map/ppermute | solution.py:27

commit v4 on v1

--- a/solution.py
+++ b/solution.py
@@ -1,3 +1,5 @@
+import math
+
 import jax
 import jax.numpy as jnp
 from jax import lax
@@ -14,6 +16,7 @@
 time_step = 0.2
 offsets_list = ((0, 1), (1, -1), (1, 0), (1, 1), (0, -1), (-1, 1), (-1, 0), (-1, -1))
 LANES = 128
+SCALE = math.sqrt(0.5 * math.log2(math.e))
 
 
 def passed_along(value, axis, steps):
@@ -68,8 +71,8 @@
                     f = jnp.broadcast_to(flags[oi - 1 : oi], (8, LANES))
                     f2 = 2.0 * f
                     fh = 0.5 * f
-                xs = jnp.broadcast_to(own[0:1] - dx * spacing, (8, LANES))
-                ys = jnp.broadcast_to(own[1:2] - dy * spacing, (8, LANES))
+                xs = jnp.broadcast_to(own[0:1] - dx * spacing * SCALE, (8, LANES))
+                ys = jnp.broadcast_to(own[1:2] - dy * spacing * SCALE, (8, LANES))
                 zs = jnp.broadcast_to(own[2:3], (8, LANES))
                 for r in range(ATOMS // 8):
                     cx = cbuf[slot, 0, n, r * 8 : (r + 1) * 8, :]
@@ -78,15 +81,13 @@
                     ddx = xs - cx
                     ddy = ys - cy
                     ddz = zs - cz
-                    s = ddx * ddx + ddy * ddy + ddz * ddz
-                    a = jnp.exp(-0.5 * s)
-                    a2 = a * a
-                    w = f2 * (a2 * a2) - fh * a
+                    t = -(ddx * ddx) - ddy * ddy - ddz * ddz
+                    w = f2 * jnp.exp2(4.0 * t) - fh * jnp.exp2(t)
                     acc[0] = acc[0] + w * ddx
                     acc[1] = acc[1] + w * ddy
                     acc[2] = acc[2] + w * ddz
             for c in range(3):
-                out_ref[i, c : c + 1, pl.ds(base, LANES)] = jnp.sum(acc[c], axis=0, keepdims=True)
+                out_ref[i, c : c + 1, pl.ds(base, LANES)] = jnp.sum(acc[c], axis=0, keepdims=True) * (1.0 / SCALE)
             return carry2
 
         lax.fori_loop(0, pairs, pair_body, 0)
@@ -130,8 +131,8 @@
     halo = jnp.concatenate([prev_row, widened, next_row], axis=1)
     chunks = -(-(width + 2 * ATOMS) // LANES)
     halo = jnp.pad(halo, ((0, 0), (0, 0), (0, chunks * LANES - width - 2 * ATOMS)))
-    halo = jnp.transpose(halo, (1, 0, 2))
-    own = jnp.transpose(coords, (1, 0, 2))
+    halo = jnp.transpose(halo, (1, 0, 2)) * SCALE
+    own = jnp.transpose(coords, (1, 0, 2)) * SCALE
     flags = jnp.repeat(jnp.transpose(bonds.astype(jnp.float32), (0, 2, 1)), ATOMS, axis=2)
     force = jnp.transpose(cluster_forces(own, halo, flags), (1, 0, 2))
     across = ring_shift(force, "rep", 2)

time: 144 us -> 141 us (0.979)
  the two profiles are of different devices: /device:TPU:26 before, /device:TPU:45 now
where the time goes in v4:
time: 141 us; the launch traced here: 140 us
  Pallas kernels  77.3 us (55%)
  starting transfers between devices  26.4 us (19%)
  waiting for transfers between devices  23.6 us (17%)
  local copies, waits for them, and re-layouts  9.08 us (6%)
  other arithmetic  3.01 us (2%)
    pallas_call x1, Pallas kernels, cluster_forces(): pl.pallas_call(kernel, out_shape=jax.ShapeDtypeStruct(own.shape, jnp.floa...  77.3 us
    ppermute x3, waiting for transfers between devices, ring_shift(): lax.ppermute(value, axis, [(source, (source + steps) % count) for source...  20.6 us
    ppermute x4, starting transfers between devices, passed_along(): lax.ppermute(value, axis, [(source, source + steps) for source in range(l...  18.5 us
    ppermute x3, starting transfers between devices, ring_shift(): lax.ppermute(value, axis, [(source, (source + steps) % count) for source...  7.84 us
    unnamed x12, local copies, waits for them, and re-layouts  4.26 us
    ppermute x4, waiting for transfers between devices, passed_along(): lax.ppermute(value, axis, [(source, source + steps) for source in range(l...  2.96 us
  transfers between devices with their start and end apart: 7, of which 3 were waited for; matrix products, arithmetic and copies ran while one was open for 4% of the time, Pallas kernels for 0%

profile of v4, /device:TPU:45, one launch (start us, length us, event | category | flops | bytes accessed | tf_op | source)
XLA Modules:
  0.0 140.2 jit_solution(6379105872701201189)
XLA Ops:
  0.6 0.0 copy-start.3
  0.6 1.3 copy.26
  1.9 0.1 fusion.4
  2.0 3.0 %collective-permute-start = (f32[3,16,64]{2,0,1:T(4,128)S(1)}, f32[3,16,64]{2,0,1:T(4,128)S(1)}, u32[]{:S(2)}, u32[]{:S(2)}) collective-permute-start(f32[3,16,64]{2,0,1:T(4,128)S(1)} %get-tuple-element.12), channel_id=1, source_target_pairs={{0,4},{4,8},{8,12},{12,16},{16,20},{20,24},{24,28},{1,5},{5,9},{9,... | collective-permute-start | bytes 36872 | tf_op jit(solution)/shard_map/ppermute | solution.py:25
  5.0 1.9 %collective-permute-start.1 = (f32[3,16,64]{2,0,1:T(4,128)S(1)}, f32[3,16,64]{2,0,1:T(4,128)S(1)}, u32[]{:S(2)}, u32[]{:S(2)}) collective-permute-start(f32[3,16,64]{2,0,1:T(4,128)S(1)} %get-tuple-element.11), channel_id=1, source_target_pairs={{4,0},{8,4},{12,8},{16,12},{20,16},{24,20},{28,24},{5,1},{9,5},{13... | collective-permute-start | bytes 36872 | tf_op jit(solution)/shard_map/ppermute | solution.py:25
  6.9 1.3 multiply_bitcast_fusion.refs_0_
  8.3 0.0 collective-permute-done
  8.3 3.0 %collective-permute-done.1 = f32[3,16,64]{2,0,1:T(4,128)S(1)} collective-permute-done((f32[3,16,64]{2,0,1:T(4,128)S(1)}, f32[3,16,64]{2,0,1:T(4,128)S(1)}, u32[]{:S(2)}, u32[]{:S(2)}) %collective-permute-start.1) | collective-permute-done | bytes 12320 | tf_op jit(solution)/shard_map/ppermute | solution.py:25
  11.2 0.7 concatenate.6
  12.0 4.0 %collective-permute-start.2 = (f32[3,1,2176]{2,0,1:T(4,128)S(1)}, f32[3,1,2176]{2,0,1:T(4,128)S(1)}, u32[]{:S(2)}, u32[]{:S(2)}) collective-permute-start(f32[3,1,2176]{2,0,1:T(4,128)S(1)} %get-tuple-element.9), channel_id=1, source_target_pairs={{0,32},{32,64},{64,96},{96,128},{128,160},{160,192},{192,224},{224... | collective-permute-start | bytes 78344 | tf_op jit(solution)/shard_map/ppermute | solution.py:25
  16.0 9.6 %collective-permute-start.3 = (f32[3,1,2176]{2,0,1:T(4,128)S(1)}, f32[3,1,2176]{2,0,1:T(4,128)S(1)}, u32[]{:S(2)}, u32[]{:S(2)}) collective-permute-start(f32[3,1,2176]{2,0,1:T(4,128)S(1)} %get-tuple-element.10), channel_id=1, source_target_pairs={{32,0},{64,32},{96,64},{128,96},{160,128},{192,160},{224,192},{256... | collective-permute-start | bytes 78344 | tf_op jit(solution)/shard_map/ppermute | solution.py:25
  25.6 0.0 copy-done.3
  25.6 1.9 %broadcast_in_dim.4 = f32[16,8,32,64]{3,2,1,0:T(8,128)} broadcast(f32[16,8,32]{2,1,0:T(8,128)S(1)} %convert_bitcast_fusion), dimensions={0,1,2} | broadcast | bytes 1064960 | tf_op jit(solution)/shard_map/broadcast_in_dim | solution.py:136
  27.6 2.1 %reshape.10.refs_2_ = f32[16,8,2048]{2,1,0:T(8,128)S(1)} reshape(f32[16,8,32,64]{3,2,1,0:T(8,128)} %broadcast_in_dim.4) | data formatting | bytes 2097152 | tf_op jit(solution)/shard_map/reshape | solution.py:136
  29.7 0.0 collective-permute-done.2
  29.7 0.0 collective-permute-done.3
  29.7 0.2 fusion.refs_1_
  29.9 0.0 copy-start
  29.9 0.0 copy-start.1
  29.9 0.0 copy-start.2
  29.9 77.3 %shard_map.67 = f32[16,3,2048]{2,1,0:T(4,128)S(1)} custom-call(f32[16,3,2048]{2,1,0:T(4,128)S(1)} %multiply_bitcast_fusion.refs_0_, f32[18,3,2176]{2,1,0:T(4,128)S(1)} %fusion.refs_1_, f32[16,8,2048]{2,1,0:T(8,128)S(1)} %reshape.10.refs_2_), custom_call_target="tpu_custom_call" | custom-call | flops 377487360 | bytes 2305024 | tf_op jit(solution)/shard_map/pallas_call | solution.py:106
  107.3 2.1 %collective-permute-start.4 = (f32[3,16,2048]{2,0,1:T(4,128)S(1)}, f32[3,16,2048]{2,0,1:T(4,128)S(1)}, u32[]{:S(2)}, u32[]{:S(2)}) collective-permute-start(f32[3,16,2048]{2,0,1:T(4,128)S(1)} %bitcast.21), channel_id=1, source_target_pairs={{0,2},{1,3},{2,0},{3,1},{4,6},{5,7},{6,4},{7,5},{8,10},{9,11},{10,... | collective-permute-start | bytes 1179656 | tf_op jit(solution)/shard_map/ppermute | solution.py:30
  109.4 3.7 %collective-permute-start.5 = (f32[3,16,2048]{2,0,1:T(4,128)S(1)}, f32[3,16,2048]{2,0,1:T(4,128)S(1)}, u32[]{:S(2)}, u32[]{:S(2)}) collective-permute-start(f32[3,16,2048]{2,0,1:T(4,128)S(1)} %bitcast.22), channel_id=1, source_target_pairs={{0,1},{1,2},{2,3},{3,0},{4,5},{5,6},{6,7},{7,4},{8,9},{9,10},{10,1... | collective-permute-start | bytes 1179656 | tf_op jit(solution)/shard_map/ppermute | solution.py:30
  113.2 2.0 %collective-permute-start.6 = (f32[3,16,2048]{2,0,1:T(4,128)S(1)}, f32[3,16,2048]{2,0,1:T(4,128)S(1)}, u32[]{:S(2)}, u32[]{:S(2)}) collective-permute-start(f32[3,16,2048]{2,0,1:T(4,128)S(1)} %bitcast.23), channel_id=1, source_target_pairs={{0,3},{1,0},{2,1},{3,2},{4,7},{5,4},{6,5},{7,6},{8,11},{9,8},{10,9... | collective-permute-start | bytes 1179656 | tf_op jit(solution)/shard_map/ppermute | solution.py:30
  115.1 8.3 %collective-permute-done.4 = f32[3,16,2048]{2,0,1:T(4,128)S(1)} collective-permute-done((f32[3,16,2048]{2,0,1:T(4,128)S(1)}, f32[3,16,2048]{2,0,1:T(4,128)S(1)}, u32[]{:S(2)}, u32[]{:S(2)}) %collective-permute-start.4) | collective-permute-done | bytes 393248 | tf_op jit(solution)/shard_map/ppermute | solution.py:30
  123.4 12.3 %collective-permute-done.5 = f32[3,16,2048]{2,0,1:T(4,128)S(1)} collective-permute-done((f32[3,16,2048]{2,0,1:T(4,128)S(1)}, f32[3,16,2048]{2,0,1:T(4,128)S(1)}, u32[]{:S(2)}, u32[]{:S(2)}) %collective-permute-start.5) | collective-permute-done | bytes 393248 | tf_op jit(solution)/shard_map/ppermute | solution.py:30
  135.8 0.0 collective-permute-done.6
  135.8 1.3 copy_add_fusion
  137.1 0.1 broadcast_multiply_fusion
  137.2 1.0 copy.11
  138.2 1.0 copy.12
  139.2 1.0 copy.13
  (5 shorter events, 0.0 us)
Async XLA Ops:
  0.6 25.0 %copy-start.3 = (s32[16,32,8]{1,2,0:T(8,128)S(1)}, s32[16,32,8]{1,2,0:T(8,128)}, u32[]{:S(2)}) copy-start(s32[16,32,8]{1,2,0:T(8,128)} %param.7) | copy-start | bytes 49156
  2.0 6.2 %collective-permute-start = (f32[3,16,64]{2,0,1:T(4,128)S(1)}, f32[3,16,64]{2,0,1:T(4,128)S(1)}, u32[]{:S(2)}, u32[]{:S(2)}) collective-permute-start(f32[3,16,64]{2,0,1:T(4,128)S(1)} %get-tuple-element.12), channel_id=1, source_target_pairs={{0,4},{4,8},{8,12},{12,16},{16,20},{20,24},{24,28},{1,5},{5,9},{9,... | collective-permute-start | bytes 36872 | tf_op jit(solution)/shard_map/ppermute | solution.py:25
  5.0 6.2 %collective-permute-start.1 = (f32[3,16,64]{2,0,1:T(4,128)S(1)}, f32[3,16,64]{2,0,1:T(4,128)S(1)}, u32[]{:S(2)}, u32[]{:S(2)}) collective-permute-start(f32[3,16,64]{2,0,1:T(4,128)S(1)} %get-tuple-element.11), channel_id=1, source_target_pairs={{4,0},{8,4},{12,8},{16,12},{20,16},{24,20},{28,24},{5,1},{9,5},{13... | collective-permute-start | bytes 36872 | tf_op jit(solution)/shard_map/ppermute | solution.py:25
  12.0 17.7 %collective-permute-start.2 = (f32[3,1,2176]{2,0,1:T(4,128)S(1)}, f32[3,1,2176]{2,0,1:T(4,128)S(1)}, u32[]{:S(2)}, u32[]{:S(2)}) collective-permute-start(f32[3,1,2176]{2,0,1:T(4,128)S(1)} %get-tuple-element.9), channel_id=1, source_target_pairs={{0,32},{32,64},{64,96},{96,128},{128,160},{160,192},{192,224},{224... | collective-permute-start | bytes 78344 | tf_op jit(solution)/shard_map/ppermute | solution.py:25
  16.0 13.7 %collective-permute-start.3 = (f32[3,1,2176]{2,0,1:T(4,128)S(1)}, f32[3,1,2176]{2,0,1:T(4,128)S(1)}, u32[]{:S(2)}, u32[]{:S(2)}) collective-permute-start(f32[3,1,2176]{2,0,1:T(4,128)S(1)} %get-tuple-element.10), channel_id=1, source_target_pairs={{32,0},{64,32},{96,64},{128,96},{160,128},{192,160},{224,192},{256... | collective-permute-start | bytes 78344 | tf_op jit(solution)/shard_map/ppermute | solution.py:25
  29.9 105.9 %copy-start = (f32[1,3,16,2048]{3,2,1,0:T(8,128)S(1)}, f32[1,3,16,2048]{3,2,1,0:T(8,128)}, u32[]{:S(2)}) copy-start(f32[1,3,16,2048]{3,2,1,0:T(8,128)} %param.4) | copy-start | bytes 1179652
  29.9 105.9 %copy-start.1 = (f32[1,3,16,2048]{3,2,1,0:T(8,128)S(1)}, f32[1,3,16,2048]{3,2,1,0:T(8,128)}, u32[]{:S(2)}) copy-start(f32[1,3,16,2048]{3,2,1,0:T(8,128)} %param.6) | copy-start | bytes 1179652
  29.9 105.8 %copy-start.2 = (f32[1,3,16,2048]{3,2,1,0:T(8,128)S(1)}, f32[1,3,16,2048]{3,2,1,0:T(8,128)}, u32[]{:S(2)}) copy-start(f32[1,3,16,2048]{3,2,1,0:T(8,128)} %param.5) | copy-start | bytes 1179652
  107.3 16.2 %collective-permute-start.4 = (f32[3,16,2048]{2,0,1:T(4,128)S(1)}, f32[3,16,2048]{2,0,1:T(4,128)S(1)}, u32[]{:S(2)}, u32[]{:S(2)}) collective-permute-start(f32[3,16,2048]{2,0,1:T(4,128)S(1)} %bitcast.21), channel_id=1, source_target_pairs={{0,2},{1,3},{2,0},{3,1},{4,6},{5,7},{6,4},{7,5},{8,10},{9,11},{10,... | collective-permute-start | bytes 1179656 | tf_op jit(solution)/shard_map/ppermute | solution.py:30
  109.4 26.3 %collective-permute-start.5 = (f32[3,16,2048]{2,0,1:T(4,128)S(1)}, f32[3,16,2048]{2,0,1:T(4,128)S(1)}, u32[]{:S(2)}, u32[]{:S(2)}) collective-permute-start(f32[3,16,2048]{2,0,1:T(4,128)S(1)} %bitcast.22), channel_id=1, source_target_pairs={{0,1},{1,2},{2,3},{3,0},{4,5},{5,6},{6,7},{7,4},{8,9},{9,10},{10,1... | collective-permute-start | bytes 1179656 | tf_op jit(solution)/shard_map/ppermute | solution.py:30
  113.2 22.6 %collective-permute-start.6 = (f32[3,16,2048]{2,0,1:T(4,128)S(1)}, f32[3,16,2048]{2,0,1:T(4,128)S(1)}, u32[]{:S(2)}, u32[]{:S(2)}) collective-permute-start(f32[3,16,2048]{2,0,1:T(4,128)S(1)} %bitcast.23), channel_id=1, source_target_pairs={{0,3},{1,0},{2,1},{3,2},{4,7},{5,4},{6,5},{7,6},{8,11},{9,8},{10,9... | collective-permute-start | bytes 1179656 | tf_op jit(solution)/shard_map/ppermute | solution.py:30

commit v5 on v4

--- a/solution.py
+++ b/solution.py
@@ -135,10 +135,8 @@
     own = jnp.transpose(coords, (1, 0, 2)) * SCALE
     flags = jnp.repeat(jnp.transpose(bonds.astype(jnp.float32), (0, 2, 1)), ATOMS, axis=2)
     force = jnp.transpose(cluster_forces(own, halo, flags), (1, 0, 2))
-    across = ring_shift(force, "rep", 2)
-    near = ring_shift(force, "rep", 1)
-    far = ring_shift(force, "rep", 3)
-    summed_force = (force + across) + (near + far)
+    gathered = lax.all_gather(force, "rep")
+    summed_force = (gathered[0] + gathered[2]) + (gathered[1] + gathered[3])
     mean_force = summed_force / lax.axis_size("rep")
     new_velocity = friction * velocities + time_step * mean_force[None] + noise_coef * noise
     new_position = positions + time_step * new_velocity

time: 141 us -> 156 us (1.11)
  the two profiles are of different devices: /device:TPU:45 before, /device:TPU:1 now
where the time goes in v5:
time: 156 us
  Pallas kernels  77.3 us (50%)
  waiting for transfers between devices  37.2 us (24%)
  starting transfers between devices  15.4 us (10%)
  between operations  14.2 us (9%)
  local copies, waits for them, and re-layouts  7.09 us (5%)
  other arithmetic  4.74 us (3%)
    pallas_call x1, Pallas kernels, cluster_forces(): pl.pallas_call(kernel, out_shape=jax.ShapeDtypeStruct(own.shape, jnp.floa...  77.3 us
    all_gather x1, waiting for transfers between devices, per_device(): gathered = lax.all_gather(force, 'rep')  36.8 us
    ppermute x4, starting transfers between devices, passed_along(): lax.ppermute(value, axis, [(source, source + steps) for source in range(l...  15.4 us
  transfers between devices with their start and end apart: 5, of which 2 were waited for; matrix products, arithmetic and copies ran while one was open for 3% of the time, Pallas kernels for 0%

profile of v5, /device:TPU:1, one launch (start us, length us, event | category | flops | bytes accessed | tf_op | source)
XLA Modules:
  0.0 155.9 jit_solution(2650042712048206994)
XLA Ops:
  7.2 0.0 copy-start.3
  7.2 0.0 all-gather.3.cloned.1.call-start
  7.2 1.3 copy.19
  8.5 0.1 fusion.6
  8.6 5.6 %collective-permute-start = (f32[3,16,64]{2,0,1:T(4,128)S(1)}, f32[3,16,64]{2,0,1:T(4,128)S(1)}, u32[]{:S(2)}, u32[]{:S(2)}) collective-permute-start(f32[3,16,64]{2,0,1:T(4,128)S(1)} %get-tuple-element.12), channel_id=1, source_target_pairs={{0,4},{4,8},{8,12},{12,16},{16,20},{20,24},{24,28},{1,5},{5,9},{9,... | collective-permute-start | bytes 36872 | tf_op jit(solution)/shard_map/ppermute | solution.py:25
  14.2 4.5 %collective-permute-start.1 = (f32[3,16,64]{2,0,1:T(4,128)S(1)}, f32[3,16,64]{2,0,1:T(4,128)S(1)}, u32[]{:S(2)}, u32[]{:S(2)}) collective-permute-start(f32[3,16,64]{2,0,1:T(4,128)S(1)} %get-tuple-element.11), channel_id=1, source_target_pairs={{4,0},{8,4},{12,8},{16,12},{20,16},{24,20},{28,24},{5,1},{9,5},{13... | collective-permute-start | bytes 36872 | tf_op jit(solution)/shard_map/ppermute | solution.py:25
  18.7 1.3 multiply_bitcast_fusion.refs_0_
  20.0 0.0 collective-permute-done
  20.0 0.3 collective-permute-done.1
  20.3 0.7 concatenate.6
  21.1 4.0 %collective-permute-start.2 = (f32[3,1,2176]{2,0,1:T(4,128)S(1)}, f32[3,1,2176]{2,0,1:T(4,128)S(1)}, u32[]{:S(2)}, u32[]{:S(2)}) collective-permute-start(f32[3,1,2176]{2,0,1:T(4,128)S(1)} %get-tuple-element.9), channel_id=1, source_target_pairs={{0,32},{32,64},{64,96},{96,128},{128,160},{160,192},{192,224},{224... | collective-permute-start | bytes 78344 | tf_op jit(solution)/shard_map/ppermute | solution.py:25
  25.1 1.3 collective-permute-start.3
  26.4 0.0 copy-done.3
  26.4 1.9 %broadcast_in_dim.4 = f32[16,8,32,64]{3,2,1,0:T(8,128)} broadcast(f32[16,8,32]{2,1,0:T(8,128)S(1)} %convert_bitcast_fusion), dimensions={0,1,2} | broadcast | bytes 1064960 | tf_op jit(solution)/shard_map/broadcast_in_dim | solution.py:136
  28.3 2.1 %reshape.15.refs_2_ = f32[16,8,2048]{2,1,0:T(8,128)S(1)} reshape(f32[16,8,32,64]{3,2,1,0:T(8,128)} %broadcast_in_dim.4) | data formatting | bytes 2097152 | tf_op jit(solution)/shard_map/reshape | solution.py:136
  30.4 0.0 collective-permute-done.2
  30.4 0.0 collective-permute-done.3
  30.4 0.2 fusion.refs_1_
  30.6 77.3 %shard_map.67 = f32[16,3,2048]{2,1,0:T(4,128)S(1)} custom-call(f32[16,3,2048]{2,1,0:T(4,128)S(1)} %multiply_bitcast_fusion.refs_0_, f32[18,3,2176]{2,1,0:T(4,128)S(1)} %fusion.refs_1_, f32[16,8,2048]{2,1,0:T(8,128)S(1)} %reshape.15.refs_2_), custom_call_target="tpu_custom_call" | custom-call | flops 377487360 | bytes 2305024 | tf_op jit(solution)/shard_map/pallas_call | solution.py:106
  108.0 0.0 copy-start
  108.0 0.0 copy-start.1
  108.0 0.0 copy-start.2
  108.0 1.0 copy.15
  109.0 0.0 all-gather.3.cloned.1.call-update
  109.0 36.8 %all-gather.3.cloned.1.call-done = f32[12,16,2048]{2,1,0:T(8,128)} async-done(((f32[3,16,2048]{2,1,0:T(8,128)}), f32[12,16,2048]{2,1,0:T(8,128)}) %all-gather.3.cloned.1.call-update) | async-done | bytes 1572880 | tf_op jit(solution)/shard_map/all_gather | solution.py:138
  145.9 0.0 copy-done
  145.9 0.0 copy-done.1
  145.9 0.0 copy-done.2
  145.9 2.4 %multiply_add_fusion = (f32[1,3,16,2048]{3,2,1,0:T(8,128)}, f32[1,3,16,2048]{3,2,1,0:T(8,128)}, f32[3,16,2048]{2,1,0:T(8,128)S(1)}) fusion(f32[1,3,16,2048]{3,2,1,0:T(8,128)S(1)} %copy-done, f32[1,3,16,2048]{3,2,1,0:T(8,128)S(1)} %copy-done.1, f32[1,3,16,2048]{3,2,1,0:T(8,128)S(1)} %copy-done.2, f32[12,16,2048]{2,1,0:T(8,128)} %all-gather.3.cloned.1.call-done), kind=kLoop, calls=%fused_computation.9 | loop fusion | flops 983040 | bytes 3932160 | tf_op jit(solution)/shard_map/add | solution.py:142
  148.3 0.8 broadcast_multiply_fusion
  (2 shorter events, 0.0 us)
Async XLA Ops:
  7.2 19.2 %copy-start.3 = (s32[16,32,8]{1,2,0:T(8,128)S(1)}, s32[16,32,8]{1,2,0:T(8,128)}, u32[]{:S(2)}) copy-start(s32[16,32,8]{1,2,0:T(8,128)} %param.7) | copy-start | bytes 49156
  7.2 138.7 %all-gather.3.cloned.1.call-start = ((), (), s32[]{:S(2)}) async-start(), calls=%async_computation | async-start | bytes 1966080 | tf_op jit(solution)/shard_map/all_gather | solution.py:138
  8.6 11.4 %collective-permute-start = (f32[3,16,64]{2,0,1:T(4,128)S(1)}, f32[3,16,64]{2,0,1:T(4,128)S(1)}, u32[]{:S(2)}, u32[]{:S(2)}) collective-permute-start(f32[3,16,64]{2,0,1:T(4,128)S(1)} %get-tuple-element.12), channel_id=1, source_target_pairs={{0,4},{4,8},{8,12},{12,16},{16,20},{20,24},{24,28},{1,5},{5,9},{9,... | collective-permute-start | bytes 36872 | tf_op jit(solution)/shard_map/ppermute | solution.py:25
  14.2 6.1 %collective-permute-start.1 = (f32[3,16,64]{2,0,1:T(4,128)S(1)}, f32[3,16,64]{2,0,1:T(4,128)S(1)}, u32[]{:S(2)}, u32[]{:S(2)}) collective-permute-start(f32[3,16,64]{2,0,1:T(4,128)S(1)} %get-tuple-element.11), channel_id=1, source_target_pairs={{4,0},{8,4},{12,8},{16,12},{20,16},{24,20},{28,24},{5,1},{9,5},{13... | collective-permute-start | bytes 36872 | tf_op jit(solution)/shard_map/ppermute | solution.py:25
  21.1 9.4 %collective-permute-start.2 = (f32[3,1,2176]{2,0,1:T(4,128)S(1)}, f32[3,1,2176]{2,0,1:T(4,128)S(1)}, u32[]{:S(2)}, u32[]{:S(2)}) collective-permute-start(f32[3,1,2176]{2,0,1:T(4,128)S(1)} %get-tuple-element.9), channel_id=1, source_target_pairs={{0,32},{32,64},{64,96},{96,128},{128,160},{160,192},{192,224},{224... | collective-permute-start | bytes 78344 | tf_op jit(solution)/shard_map/ppermute | solution.py:25
  25.1 5.4 %collective-permute-start.3 = (f32[3,1,2176]{2,0,1:T(4,128)S(1)}, f32[3,1,2176]{2,0,1:T(4,128)S(1)}, u32[]{:S(2)}, u32[]{:S(2)}) collective-permute-start(f32[3,1,2176]{2,0,1:T(4,128)S(1)} %get-tuple-element.10), channel_id=1, source_target_pairs={{32,0},{64,32},{96,64},{128,96},{160,128},{192,160},{224,192},{256... | collective-permute-start | bytes 78344 | tf_op jit(solution)/shard_map/ppermute | solution.py:25
  108.0 37.9 %copy-start = (f32[1,3,16,2048]{3,2,1,0:T(8,128)S(1)}, f32[1,3,16,2048]{3,2,1,0:T(8,128)}, u32[]{:S(2)}) copy-start(f32[1,3,16,2048]{3,2,1,0:T(8,128)} %param.4) | copy-start | bytes 1179652
  108.0 37.9 %copy-start.1 = (f32[1,3,16,2048]{3,2,1,0:T(8,128)S(1)}, f32[1,3,16,2048]{3,2,1,0:T(8,128)}, u32[]{:S(2)}) copy-start(f32[1,3,16,2048]{3,2,1,0:T(8,128)} %param.6) | copy-start | bytes 1179652
  108.0 37.9 %copy-start.2 = (f32[1,3,16,2048]{3,2,1,0:T(8,128)S(1)}, f32[1,3,16,2048]{3,2,1,0:T(8,128)}, u32[]{:S(2)}) copy-start(f32[1,3,16,2048]{3,2,1,0:T(8,128)} %param.5) | copy-start | bytes 1179652
Sparse Core Ops, SparseCore 0:
  109.1 36.6 all-gather.2

commit v6 on v4

--- a/solution.py
+++ b/solution.py
@@ -86,8 +86,12 @@
                     acc[0] = acc[0] + w * ddx
                     acc[1] = acc[1] + w * ddy
                     acc[2] = acc[2] + w * ddz
+            block = pl.multiple_of((i // 8) * 8, 8)
+            mine = lax.broadcasted_iota(jnp.int32, (8, LANES), 0) == i % 8
             for c in range(3):
-                out_ref[i, c : c + 1, pl.ds(base, LANES)] = jnp.sum(acc[c], axis=0, keepdims=True) * (1.0 / SCALE)
+                row = jnp.sum(acc[c], axis=0, keepdims=True) * (1.0 / SCALE)
+                held = out_ref[c, pl.ds(block, 8), pl.ds(base, LANES)]
+                out_ref[c, pl.ds(block, 8), pl.ds(base, LANES)] = jnp.where(mine, row, held)
             return carry2
 
         lax.fori_loop(0, pairs, pair_body, 0)
@@ -105,7 +109,7 @@
     pair_count = rows * pairs * 9 * ATOMS * LANES
     return pl.pallas_call(
         kernel,
-        out_shape=jax.ShapeDtypeStruct(own.shape, jnp.float32),
+        out_shape=jax.ShapeDtypeStruct((3, rows, width), jnp.float32),
         in_specs=[pl.BlockSpec(memory_space=pltpu.VMEM)] * 3,
         out_specs=pl.BlockSpec(memory_space=pltpu.VMEM),
         scratch_shapes=[pltpu.VMEM((3, 3, n_blocks, ATOMS, LANES), jnp.float32)],
@@ -134,7 +138,7 @@
     halo = jnp.transpose(halo, (1, 0, 2)) * SCALE
     own = jnp.transpose(coords, (1, 0, 2)) * SCALE
     flags = jnp.repeat(jnp.transpose(bonds.astype(jnp.float32), (0, 2, 1)), ATOMS, axis=2)
-    force = jnp.transpose(cluster_forces(own, halo, flags), (1, 0, 2))
+    force = cluster_forces(own, halo, flags)
     across = ring_shift(force, "rep", 2)
     near = ring_shift(force, "rep", 1)
     far = ring_shift(force, "rep", 3)

time: 141 us -> 133 us (0.943)
  the two profiles are of different devices: /device:TPU:45 before, /device:TPU:41 now
where the time goes in v6:
time: 133 us
  Pallas kernels  78.4 us (59%)
  starting transfers between devices  29.7 us (22%)
  waiting for transfers between devices  14.7 us (11%)
  local copies, waits for them, and re-layouts  6.15 us (5%)
  other arithmetic  3.43 us (3%)
    pallas_call x1, Pallas kernels, cluster_forces(): pl.pallas_call(kernel, out_shape=jax.ShapeDtypeStruct((3, rows, width), j...  78.4 us
    ppermute x4, starting transfers between devices, passed_along(): lax.ppermute(value, axis, [(source, source + steps) for source in range(l...  18.5 us
    ppermute x3, waiting for transfers between devices, ring_shift(): lax.ppermute(value, axis, [(source, (source + steps) % count) for source...  11.7 us
    ppermute x3, starting transfers between devices, ring_shift(): lax.ppermute(value, axis, [(source, (source + steps) % count) for source...  11.1 us
    ppermute x4, waiting for transfers between devices, passed_along(): lax.ppermute(value, axis, [(source, source + steps) for source in range(l...  2.96 us
  transfers between devices with their start and end apart: 7, of which 3 were waited for; matrix products, arithmetic and copies ran while one was open for 4% of the time, Pallas kernels for 0%

profile of v6, /device:TPU:41, one launch (start us, length us, event | category | flops | bytes accessed | tf_op | source)
XLA Modules:
  0.0 133.1 jit_solution(13080994398666964811)
XLA Ops:
  0.6 0.0 copy-start.3
  0.6 1.3 copy.11
  1.9 0.1 fusion.4
  2.0 3.0 %collective-permute-start = (f32[3,16,64]{2,0,1:T(4,128)S(1)}, f32[3,16,64]{2,0,1:T(4,128)S(1)}, u32[]{:S(2)}, u32[]{:S(2)}) collective-permute-start(f32[3,16,64]{2,0,1:T(4,128)S(1)} %get-tuple-element.9), channel_id=1, source_target_pairs={{0,4},{4,8},{8,12},{12,16},{16,20},{20,24},{24,28},{1,5},{5,9},{9,... | collective-permute-start | bytes 36872 | tf_op jit(solution)/shard_map/ppermute | solution.py:25
  5.0 1.9 %collective-permute-start.1 = (f32[3,16,64]{2,0,1:T(4,128)S(1)}, f32[3,16,64]{2,0,1:T(4,128)S(1)}, u32[]{:S(2)}, u32[]{:S(2)}) collective-permute-start(f32[3,16,64]{2,0,1:T(4,128)S(1)} %get-tuple-element.8), channel_id=1, source_target_pairs={{4,0},{8,4},{12,8},{16,12},{20,16},{24,20},{28,24},{5,1},{9,5},{13... | collective-permute-start | bytes 36872 | tf_op jit(solution)/shard_map/ppermute | solution.py:25
  6.9 1.3 %multiply_bitcast_fusion.refs_0_ = f32[16,3,2048]{2,1,0:T(4,128)S(1)} fusion(f32[1,3,16,2048]{3,2,1,0:T(8,128)} %param.4), kind=kLoop, calls=%fused_computation.3 | loop fusion | flops 98304 | bytes 786432 | tf_op jit(solution)/shard_map/mul | solution.py:139
  8.3 0.0 collective-permute-done
  8.3 3.0 %collective-permute-done.1 = f32[3,16,64]{2,0,1:T(4,128)S(1)} collective-permute-done((f32[3,16,64]{2,0,1:T(4,128)S(1)}, f32[3,16,64]{2,0,1:T(4,128)S(1)}, u32[]{:S(2)}, u32[]{:S(2)}) %collective-permute-start.1) | collective-permute-done | bytes 12320 | tf_op jit(solution)/shard_map/ppermute | solution.py:25
  11.2 0.7 concatenate.6
  12.0 4.0 %collective-permute-start.2 = (f32[3,1,2176]{2,0,1:T(4,128)S(1)}, f32[3,1,2176]{2,0,1:T(4,128)S(1)}, u32[]{:S(2)}, u32[]{:S(2)}) collective-permute-start(f32[3,1,2176]{2,0,1:T(4,128)S(1)} %get-tuple-element.6), channel_id=1, source_target_pairs={{0,32},{32,64},{64,96},{96,128},{128,160},{160,192},{192,224},{224... | collective-permute-start | bytes 78344 | tf_op jit(solution)/shard_map/ppermute | solution.py:25
  16.0 9.6 %collective-permute-start.3 = (f32[3,1,2176]{2,0,1:T(4,128)S(1)}, f32[3,1,2176]{2,0,1:T(4,128)S(1)}, u32[]{:S(2)}, u32[]{:S(2)}) collective-permute-start(f32[3,1,2176]{2,0,1:T(4,128)S(1)} %get-tuple-element.7), channel_id=1, source_target_pairs={{32,0},{64,32},{96,64},{128,96},{160,128},{192,160},{224,192},{256... | collective-permute-start | bytes 78344 | tf_op jit(solution)/shard_map/ppermute | solution.py:25
  25.6 0.0 copy-done.3
  25.6 1.9 %broadcast_in_dim.4 = f32[16,8,32,64]{3,2,1,0:T(8,128)} broadcast(f32[16,8,32]{2,1,0:T(8,128)S(1)} %convert_bitcast_fusion), dimensions={0,1,2} | broadcast | bytes 1064960 | tf_op jit(solution)/shard_map/broadcast_in_dim | solution.py:140
  27.6 2.1 %reshape.10.refs_2_ = f32[16,8,2048]{2,1,0:T(8,128)S(1)} reshape(f32[16,8,32,64]{3,2,1,0:T(8,128)} %broadcast_in_dim.4) | data formatting | bytes 2097152 | tf_op jit(solution)/shard_map/reshape | solution.py:140
  29.7 0.0 collective-permute-done.2
  29.7 0.0 collective-permute-done.3
  29.7 0.2 fusion.refs_1_
  29.9 0.0 copy-start
  29.9 0.0 copy-start.1
  29.9 0.0 copy-start.2
  29.9 78.4 %shard_map.67 = f32[3,16,2048]{2,1,0:T(8,128)S(1)} custom-call(f32[16,3,2048]{2,1,0:T(4,128)S(1)} %multiply_bitcast_fusion.refs_0_, f32[18,3,2176]{2,1,0:T(4,128)S(1)} %fusion.refs_1_, f32[16,8,2048]{2,1,0:T(8,128)S(1)} %reshape.10.refs_2_), custom_call_target="tpu_custom_call" | custom-call | flops 377487360 | bytes 2305024 | tf_op jit(solution)/shard_map/pallas_call | solution.py:110
  108.4 4.7 %collective-permute-start.4 = (f32[3,16,2048]{2,1,0:T(8,128)S(1)}, f32[3,16,2048]{2,1,0:T(8,128)S(1)}, u32[]{:S(2)}, u32[]{:S(2)}) collective-permute-start(f32[3,16,2048]{2,1,0:T(8,128)S(1)} %shard_map.67), channel_id=1, source_target_pairs={{0,2},{1,3},{2,0},{3,1},{4,6},{5,7},{6,4},{7,5},{8,10},{9,11},{10,... | collective-permute-start | bytes 1179656 | tf_op jit(solution)/shard_map/ppermute | solution.py:30
  113.0 2.2 %collective-permute-start.5 = (f32[3,16,2048]{2,1,0:T(8,128)S(1)}, f32[3,16,2048]{2,1,0:T(8,128)S(1)}, u32[]{:S(2)}, u32[]{:S(2)}) collective-permute-start(f32[3,16,2048]{2,1,0:T(8,128)S(1)} %shard_map.67), channel_id=1, source_target_pairs={{0,1},{1,2},{2,3},{3,0},{4,5},{5,6},{6,7},{7,4},{8,9},{9,10},{10,1... | collective-permute-start | bytes 1179656 | tf_op jit(solution)/shard_map/ppermute | solution.py:30
  115.3 4.3 %collective-permute-start.6 = (f32[3,16,2048]{2,1,0:T(8,128)S(1)}, f32[3,16,2048]{2,1,0:T(8,128)S(1)}, u32[]{:S(2)}, u32[]{:S(2)}) collective-permute-start(f32[3,16,2048]{2,1,0:T(8,128)S(1)} %shard_map.67), channel_id=1, source_target_pairs={{0,3},{1,0},{2,1},{3,2},{4,7},{5,4},{6,5},{7,6},{8,11},{9,8},{10,9... | collective-permute-start | bytes 1179656 | tf_op jit(solution)/shard_map/ppermute | solution.py:30
  119.5 2.2 %collective-permute-done.4 = f32[3,16,2048]{2,1,0:T(8,128)S(1)} collective-permute-done((f32[3,16,2048]{2,1,0:T(8,128)S(1)}, f32[3,16,2048]{2,1,0:T(8,128)S(1)}, u32[]{:S(2)}, u32[]{:S(2)}) %collective-permute-start.4) | collective-permute-done | bytes 393248 | tf_op jit(solution)/shard_map/ppermute | solution.py:30
  121.7 9.5 %collective-permute-done.5 = f32[3,16,2048]{2,1,0:T(8,128)S(1)} collective-permute-done((f32[3,16,2048]{2,1,0:T(8,128)S(1)}, f32[3,16,2048]{2,1,0:T(8,128)S(1)}, u32[]{:S(2)}, u32[]{:S(2)}) %collective-permute-start.5) | collective-permute-done | bytes 393248 | tf_op jit(solution)/shard_map/ppermute | solution.py:30
  131.2 0.0 collective-permute-done.6
  131.2 0.0 copy-done
  131.2 0.0 copy-done.1
  131.2 0.0 copy-done.2
  131.3 1.1 multiply_add_fusion
  132.4 0.8 broadcast_multiply_fusion
  (2 shorter events, 0.0 us)
Async XLA Ops:
  0.6 25.0 %copy-start.3 = (s32[16,32,8]{1,2,0:T(8,128)S(1)}, s32[16,32,8]{1,2,0:T(8,128)}, u32[]{:S(2)}) copy-start(s32[16,32,8]{1,2,0:T(8,128)} %param.7) | copy-start | bytes 49156
  2.0 6.2 %collective-permute-start = (f32[3,16,64]{2,0,1:T(4,128)S(1)}, f32[3,16,64]{2,0,1:T(4,128)S(1)}, u32[]{:S(2)}, u32[]{:S(2)}) collective-permute-start(f32[3,16,64]{2,0,1:T(4,128)S(1)} %get-tuple-element.9), channel_id=1, source_target_pairs={{0,4},{4,8},{8,12},{12,16},{16,20},{20,24},{24,28},{1,5},{5,9},{9,... | collective-permute-start | bytes 36872 | tf_op jit(solution)/shard_map/ppermute | solution.py:25
  5.0 6.2 %collective-permute-start.1 = (f32[3,16,64]{2,0,1:T(4,128)S(1)}, f32[3,16,64]{2,0,1:T(4,128)S(1)}, u32[]{:S(2)}, u32[]{:S(2)}) collective-permute-start(f32[3,16,64]{2,0,1:T(4,128)S(1)} %get-tuple-element.8), channel_id=1, source_target_pairs={{4,0},{8,4},{12,8},{16,12},{20,16},{24,20},{28,24},{5,1},{9,5},{13... | collective-permute-start | bytes 36872 | tf_op jit(solution)/shard_map/ppermute | solution.py:25
  12.0 17.7 %collective-permute-start.2 = (f32[3,1,2176]{2,0,1:T(4,128)S(1)}, f32[3,1,2176]{2,0,1:T(4,128)S(1)}, u32[]{:S(2)}, u32[]{:S(2)}) collective-permute-start(f32[3,1,2176]{2,0,1:T(4,128)S(1)} %get-tuple-element.6), channel_id=1, source_target_pairs={{0,32},{32,64},{64,96},{96,128},{128,160},{160,192},{192,224},{224... | collective-permute-start | bytes 78344 | tf_op jit(solution)/shard_map/ppermute | solution.py:25
  16.0 13.7 %collective-permute-start.3 = (f32[3,1,2176]{2,0,1:T(4,128)S(1)}, f32[3,1,2176]{2,0,1:T(4,128)S(1)}, u32[]{:S(2)}, u32[]{:S(2)}) collective-permute-start(f32[3,1,2176]{2,0,1:T(4,128)S(1)} %get-tuple-element.7), channel_id=1, source_target_pairs={{32,0},{64,32},{96,64},{128,96},{160,128},{192,160},{224,192},{256... | collective-permute-start | bytes 78344 | tf_op jit(solution)/shard_map/ppermute | solution.py:25
  29.9 101.3 %copy-start = (f32[1,3,16,2048]{3,2,1,0:T(8,128)S(1)}, f32[1,3,16,2048]{3,2,1,0:T(8,128)}, u32[]{:S(2)}) copy-start(f32[1,3,16,2048]{3,2,1,0:T(8,128)} %param.4) | copy-start | bytes 1179652
  29.9 101.3 %copy-start.1 = (f32[1,3,16,2048]{3,2,1,0:T(8,128)S(1)}, f32[1,3,16,2048]{3,2,1,0:T(8,128)}, u32[]{:S(2)}) copy-start(f32[1,3,16,2048]{3,2,1,0:T(8,128)} %param.6) | copy-start | bytes 1179652
  29.9 101.3 %copy-start.2 = (f32[1,3,16,2048]{3,2,1,0:T(8,128)S(1)}, f32[1,3,16,2048]{3,2,1,0:T(8,128)}, u32[]{:S(2)}) copy-start(f32[1,3,16,2048]{3,2,1,0:T(8,128)} %param.5) | copy-start | bytes 1179652
  108.4 13.3 %collective-permute-start.4 = (f32[3,16,2048]{2,1,0:T(8,128)S(1)}, f32[3,16,2048]{2,1,0:T(8,128)S(1)}, u32[]{:S(2)}, u32[]{:S(2)}) collective-permute-start(f32[3,16,2048]{2,1,0:T(8,128)S(1)} %shard_map.67), channel_id=1, source_target_pairs={{0,2},{1,3},{2,0},{3,1},{4,6},{5,7},{6,4},{7,5},{8,10},{9,11},{10,... | collective-permute-start | bytes 1179656 | tf_op jit(solution)/shard_map/ppermute | solution.py:30
  113.0 18.2 %collective-permute-start.5 = (f32[3,16,2048]{2,1,0:T(8,128)S(1)}, f32[3,16,2048]{2,1,0:T(8,128)S(1)}, u32[]{:S(2)}, u32[]{:S(2)}) collective-permute-start(f32[3,16,2048]{2,1,0:T(8,128)S(1)} %shard_map.67), channel_id=1, source_target_pairs={{0,1},{1,2},{2,3},{3,0},{4,5},{5,6},{6,7},{7,4},{8,9},{9,10},{10,1... | collective-permute-start | bytes 1179656 | tf_op jit(solution)/shard_map/ppermute | solution.py:30
  115.3 16.0 %collective-permute-start.6 = (f32[3,16,2048]{2,1,0:T(8,128)S(1)}, f32[3,16,2048]{2,1,0:T(8,128)S(1)}, u32[]{:S(2)}, u32[]{:S(2)}) collective-permute-start(f32[3,16,2048]{2,1,0:T(8,128)S(1)} %shard_map.67), channel_id=1, source_target_pairs={{0,3},{1,0},{2,1},{3,2},{4,7},{5,4},{6,5},{7,6},{8,11},{9,8},{10,9... | collective-permute-start | bytes 1179656 | tf_op jit(solution)/shard_map/ppermute | solution.py:30

commit v7 on v6

--- a/solution.py
+++ b/solution.py
@@ -137,7 +137,10 @@
     halo = jnp.pad(halo, ((0, 0), (0, 0), (0, chunks * LANES - width - 2 * ATOMS)))
     halo = jnp.transpose(halo, (1, 0, 2)) * SCALE
     own = jnp.transpose(coords, (1, 0, 2)) * SCALE
-    flags = jnp.repeat(jnp.transpose(bonds.astype(jnp.float32), (0, 2, 1)), ATOMS, axis=2)
+    spread = (lax.broadcasted_iota(jnp.int32, (cols_local, width), 1) // ATOMS
+              == lax.broadcasted_iota(jnp.int32, (cols_local, width), 0)).astype(jnp.float32)
+    per_cluster = jnp.transpose(bonds.astype(jnp.float32), (0, 2, 1)).reshape(-1, cols_local)
+    flags = jnp.dot(per_cluster, spread, precision=lax.Precision.HIGHEST).reshape(rows_local, -1, width)
     force = cluster_forces(own, halo, flags)
     across = ring_shift(force, "rep", 2)
     near = ring_shift(force, "rep", 1)

time: 133 us -> 133 us (level)
  the two profiles are of different devices: /device:TPU:41 before, /device:TPU:24 now
where the time goes in v7:
time: 133 us
  Pallas kernels  78.4 us (59%)
  starting transfers between devices  27.9 us (21%)
  waiting for transfers between devices  20.3 us (15%)
  other arithmetic  2.43 us (2%)
  local copies, waits for them, and re-layouts  2.16 us (2%)
    pallas_call x1, Pallas kernels, cluster_forces(): pl.pallas_call(kernel, out_shape=jax.ShapeDtypeStruct((3, rows, width), j...  78.4 us
    ppermute x4, starting transfers between devices, passed_along(): lax.ppermute(value, axis, [(source, source + steps) for source in range(l...  17.1 us
    ppermute x3, waiting for transfers between devices, ring_shift(): lax.ppermute(value, axis, [(source, (source + steps) % count) for source...  16 us
    ppermute x3, starting transfers between devices, ring_shift(): lax.ppermute(value, axis, [(source, (source + steps) % count) for source...  10.8 us
    ppermute x4, waiting for transfers between devices, passed_along(): lax.ppermute(value, axis, [(source, source + steps) for source in range(l...  4.33 us
  transfers between devices with their start and end apart: 7, of which 4 were waited for; matrix products, arithmetic and copies ran while one was open for 1% of the time, Pallas kernels for 0%

profile of v7, /device:TPU:24, one launch (start us, length us, event | category | flops | bytes accessed | tf_op | source)
XLA Modules:
  0.0 132.6 jit_solution(9573253743650730565)
XLA Ops:
  0.6 0.0 copy-start
  0.6 1.3 %copy.11 = f32[1,3,16,2048]{3,1,2,0:T(4,128)S(1)} copy(f32[1,3,16,2048]{3,2,1,0:T(8,128)} %param.4) | data formatting | bytes 786432 | tf_op args[0]
  2.0 0.1 fusion.12
  2.1 1.9 %collective-permute-start.1 = (f32[3,16,64]{2,0,1:T(4,128)S(1)}, f32[3,16,64]{2,0,1:T(4,128)S(1)}, u32[]{:S(2)}, u32[]{:S(2)}) collective-permute-start(f32[3,16,64]{2,0,1:T(4,128)S(1)} %get-tuple-element.8), channel_id=1, source_target_pairs={{4,0},{8,4},{12,8},{16,12},{20,16},{24,20},{28,24},{5,1},{9,5},{13... | collective-permute-start | bytes 36872 | tf_op jit(solution)/shard_map/ppermute | solution.py:25
  4.0 2.4 %collective-permute-start = (f32[3,16,64]{2,0,1:T(4,128)S(1)}, f32[3,16,64]{2,0,1:T(4,128)S(1)}, u32[]{:S(2)}, u32[]{:S(2)}) collective-permute-start(f32[3,16,64]{2,0,1:T(4,128)S(1)} %get-tuple-element.9), channel_id=1, source_target_pairs={{0,4},{4,8},{8,12},{12,16},{16,20},{20,24},{24,28},{1,5},{5,9},{9,... | collective-permute-start | bytes 36872 | tf_op jit(solution)/shard_map/ppermute | solution.py:25
  6.4 0.0 copy-done
  6.4 0.3 multiply_bitcast_fusion.refs_0_
  6.8 0.0 collective-permute-done.1
  6.8 3.3 %collective-permute-done = f32[3,16,64]{2,0,1:T(4,128)S(1)} collective-permute-done((f32[3,16,64]{2,0,1:T(4,128)S(1)}, f32[3,16,64]{2,0,1:T(4,128)S(1)}, u32[]{:S(2)}, u32[]{:S(2)}) %collective-permute-start) | collective-permute-done | bytes 12320 | tf_op jit(solution)/shard_map/ppermute | solution.py:25
  10.1 0.7 concatenate.6
  10.8 0.0 copy-start.3
  10.9 4.5 %collective-permute-start.2 = (f32[3,1,2176]{2,0,1:T(4,128)S(1)}, f32[3,1,2176]{2,0,1:T(4,128)S(1)}, u32[]{:S(2)}, u32[]{:S(2)}) collective-permute-start(f32[3,1,2176]{2,0,1:T(4,128)S(1)} %get-tuple-element.6), channel_id=1, source_target_pairs={{0,32},{32,64},{64,96},{96,128},{128,160},{160,192},{192,224},{224... | collective-permute-start | bytes 78344 | tf_op jit(solution)/shard_map/ppermute | solution.py:25
  15.4 8.3 %collective-permute-start.3 = (f32[3,1,2176]{2,0,1:T(4,128)S(1)}, f32[3,1,2176]{2,0,1:T(4,128)S(1)}, u32[]{:S(2)}, u32[]{:S(2)}) collective-permute-start(f32[3,1,2176]{2,0,1:T(4,128)S(1)} %get-tuple-element.7), channel_id=1, source_target_pairs={{32,0},{64,32},{96,64},{128,96},{160,128},{192,160},{224,192},{256... | collective-permute-start | bytes 78344 | tf_op jit(solution)/shard_map/ppermute | solution.py:25
  23.7 0.0 copy-done.3
  23.7 0.6 convolution_bitcast_fusion.refs_2_
  24.2 0.0 collective-permute-done.2
  24.2 1.0 collective-permute-done.3
  25.2 0.2 fusion.refs_1_
  25.5 0.0 copy-start.1
  25.5 0.0 copy-start.2
  25.5 78.4 %shard_map.67 = f32[3,16,2048]{2,1,0:T(8,128)S(1)} custom-call(f32[16,3,2048]{2,1,0:T(4,128)S(1)} %multiply_bitcast_fusion.refs_0_, f32[18,3,2176]{2,1,0:T(4,128)S(1)} %fusion.refs_1_, f32[16,8,2048]{2,1,0:T(8,128)S(1)} %convolution_bitcast_fusion.refs_2_), custom_call_target="tpu_custom_call" | custom-call | flops 377487360 | bytes 2305024 | tf_op jit(solution)/shard_map/pallas_call | solution.py:110
  103.9 4.7 %collective-permute-start.6 = (f32[3,16,2048]{2,1,0:T(8,128)S(1)}, f32[3,16,2048]{2,1,0:T(8,128)S(1)}, u32[]{:S(2)}, u32[]{:S(2)}) collective-permute-start(f32[3,16,2048]{2,1,0:T(8,128)S(1)} %shard_map.67), channel_id=1, source_target_pairs={{0,3},{1,0},{2,1},{3,2},{4,7},{5,4},{6,5},{7,6},{8,11},{9,8},{10,9... | collective-permute-start | bytes 1179656 | tf_op jit(solution)/shard_map/ppermute | solution.py:30
  108.6 1.9 %collective-permute-start.5 = (f32[3,16,2048]{2,1,0:T(8,128)S(1)}, f32[3,16,2048]{2,1,0:T(8,128)S(1)}, u32[]{:S(2)}, u32[]{:S(2)}) collective-permute-start(f32[3,16,2048]{2,1,0:T(8,128)S(1)} %shard_map.67), channel_id=1, source_target_pairs={{0,1},{1,2},{2,3},{3,0},{4,5},{5,6},{6,7},{7,4},{8,9},{9,10},{10,1... | collective-permute-start | bytes 1179656 | tf_op jit(solution)/shard_map/ppermute | solution.py:30
  110.5 4.2 %collective-permute-start.4 = (f32[3,16,2048]{2,1,0:T(8,128)S(1)}, f32[3,16,2048]{2,1,0:T(8,128)S(1)}, u32[]{:S(2)}, u32[]{:S(2)}) collective-permute-start(f32[3,16,2048]{2,1,0:T(8,128)S(1)} %shard_map.67), channel_id=1, source_target_pairs={{0,2},{1,3},{2,0},{3,1},{4,6},{5,7},{6,4},{7,5},{8,10},{9,11},{10,... | collective-permute-start | bytes 1179656 | tf_op jit(solution)/shard_map/ppermute | solution.py:30
  114.7 10.7 %collective-permute-done.6 = f32[3,16,2048]{2,1,0:T(8,128)S(1)} collective-permute-done((f32[3,16,2048]{2,1,0:T(8,128)S(1)}, f32[3,16,2048]{2,1,0:T(8,128)S(1)}, u32[]{:S(2)}, u32[]{:S(2)}) %collective-permute-start.6) | collective-permute-done | bytes 393248 | tf_op jit(solution)/shard_map/ppermute | solution.py:30
  125.4 5.3 %collective-permute-done.5 = f32[3,16,2048]{2,1,0:T(8,128)S(1)} collective-permute-done((f32[3,16,2048]{2,1,0:T(8,128)S(1)}, f32[3,16,2048]{2,1,0:T(8,128)S(1)}, u32[]{:S(2)}, u32[]{:S(2)}) %collective-permute-start.5) | collective-permute-done | bytes 393248 | tf_op jit(solution)/shard_map/ppermute | solution.py:30
  130.7 0.0 collective-permute-done.4
  130.7 0.0 copy-done.1
  130.7 0.0 copy-done.2
  130.7 1.1 multiply_add_fusion
  131.8 0.8 broadcast_multiply_fusion
  (3 shorter events, 0.0 us)
Async XLA Ops:
  0.6 5.8 %copy-start = (f32[1,3,16,2048]{3,2,1,0:T(8,128)S(1)}, f32[1,3,16,2048]{3,2,1,0:T(8,128)}, u32[]{:S(2)}) copy-start(f32[1,3,16,2048]{3,2,1,0:T(8,128)} %param.4) | copy-start | bytes 1179652
  2.1 4.7 %collective-permute-start.1 = (f32[3,16,64]{2,0,1:T(4,128)S(1)}, f32[3,16,64]{2,0,1:T(4,128)S(1)}, u32[]{:S(2)}, u32[]{:S(2)}) collective-permute-start(f32[3,16,64]{2,0,1:T(4,128)S(1)} %get-tuple-element.8), channel_id=1, source_target_pairs={{4,0},{8,4},{12,8},{16,12},{20,16},{24,20},{28,24},{5,1},{9,5},{13... | collective-permute-start | bytes 36872 | tf_op jit(solution)/shard_map/ppermute | solution.py:25
  4.0 6.1 %collective-permute-start = (f32[3,16,64]{2,0,1:T(4,128)S(1)}, f32[3,16,64]{2,0,1:T(4,128)S(1)}, u32[]{:S(2)}, u32[]{:S(2)}) collective-permute-start(f32[3,16,64]{2,0,1:T(4,128)S(1)} %get-tuple-element.9), channel_id=1, source_target_pairs={{0,4},{4,8},{8,12},{12,16},{16,20},{20,24},{24,28},{1,5},{5,9},{9,... | collective-permute-start | bytes 36872 | tf_op jit(solution)/shard_map/ppermute | solution.py:25
  10.8 12.8 %copy-start.3 = (s32[16,32,8]{1,2,0:T(8,128)S(1)}, s32[16,32,8]{1,2,0:T(8,128)}, u32[]{:S(2)}) copy-start(s32[16,32,8]{1,2,0:T(8,128)} %param.7) | copy-start | bytes 49156
  10.9 13.4 %collective-permute-start.2 = (f32[3,1,2176]{2,0,1:T(4,128)S(1)}, f32[3,1,2176]{2,0,1:T(4,128)S(1)}, u32[]{:S(2)}, u32[]{:S(2)}) collective-permute-start(f32[3,1,2176]{2,0,1:T(4,128)S(1)} %get-tuple-element.6), channel_id=1, source_target_pairs={{0,32},{32,64},{64,96},{96,128},{128,160},{160,192},{192,224},{224... | collective-permute-start | bytes 78344 | tf_op jit(solution)/shard_map/ppermute | solution.py:25
  15.4 9.9 %collective-permute-start.3 = (f32[3,1,2176]{2,0,1:T(4,128)S(1)}, f32[3,1,2176]{2,0,1:T(4,128)S(1)}, u32[]{:S(2)}, u32[]{:S(2)}) collective-permute-start(f32[3,1,2176]{2,0,1:T(4,128)S(1)} %get-tuple-element.7), channel_id=1, source_target_pairs={{32,0},{64,32},{96,64},{128,96},{160,128},{192,160},{224,192},{256... | collective-permute-start | bytes 78344 | tf_op jit(solution)/shard_map/ppermute | solution.py:25
  25.5 105.2 %copy-start.1 = (f32[1,3,16,2048]{3,2,1,0:T(8,128)S(1)}, f32[1,3,16,2048]{3,2,1,0:T(8,128)}, u32[]{:S(2)}) copy-start(f32[1,3,16,2048]{3,2,1,0:T(8,128)} %param.6) | copy-start | bytes 1179652
  25.5 105.2 %copy-start.2 = (f32[1,3,16,2048]{3,2,1,0:T(8,128)S(1)}, f32[1,3,16,2048]{3,2,1,0:T(8,128)}, u32[]{:S(2)}) copy-start(f32[1,3,16,2048]{3,2,1,0:T(8,128)} %param.5) | copy-start | bytes 1179652
  103.9 21.5 %collective-permute-start.6 = (f32[3,16,2048]{2,1,0:T(8,128)S(1)}, f32[3,16,2048]{2,1,0:T(8,128)S(1)}, u32[]{:S(2)}, u32[]{:S(2)}) collective-permute-start(f32[3,16,2048]{2,1,0:T(8,128)S(1)} %shard_map.67), channel_id=1, source_target_pairs={{0,3},{1,0},{2,1},{3,2},{4,7},{5,4},{6,5},{7,6},{8,11},{9,8},{10,9... | collective-permute-start | bytes 1179656 | tf_op jit(solution)/shard_map/ppermute | solution.py:30
  108.6 22.1 %collective-permute-start.5 = (f32[3,16,2048]{2,1,0:T(8,128)S(1)}, f32[3,16,2048]{2,1,0:T(8,128)S(1)}, u32[]{:S(2)}, u32[]{:S(2)}) collective-permute-start(f32[3,16,2048]{2,1,0:T(8,128)S(1)} %shard_map.67), channel_id=1, source_target_pairs={{0,1},{1,2},{2,3},{3,0},{4,5},{5,6},{6,7},{7,4},{8,9},{9,10},{10,1... | collective-permute-start | bytes 1179656 | tf_op jit(solution)/shard_map/ppermute | solution.py:30
  110.5 20.2 %collective-permute-start.4 = (f32[3,16,2048]{2,1,0:T(8,128)S(1)}, f32[3,16,2048]{2,1,0:T(8,128)S(1)}, u32[]{:S(2)}, u32[]{:S(2)}) collective-permute-start(f32[3,16,2048]{2,1,0:T(8,128)S(1)} %shard_map.67), channel_id=1, source_target_pairs={{0,2},{1,3},{2,0},{3,1},{4,6},{5,7},{6,4},{7,5},{8,10},{9,11},{10,... | collective-permute-start | bytes 1179656 | tf_op jit(solution)/shard_map/ppermute | solution.py:30

commit v8 on v7

--- a/solution.py
+++ b/solution.py
@@ -65,12 +65,12 @@
                 slot = lax.rem(i + 1 + dx, 3)
                 n = 2 * k + 1 + dy
                 if oi == 0:
-                    f2 = jnp.full((8, LANES), 2.0, jnp.float32)
-                    fh = jnp.full((8, LANES), 0.5, jnp.float32)
+                    low = jnp.full((8, LANES), -1.0, jnp.float32)
+                    high = jnp.full((8, LANES), 5.0, jnp.float32)
                 else:
-                    f = jnp.broadcast_to(flags[oi - 1 : oi], (8, LANES))
-                    f2 = 2.0 * f
-                    fh = 0.5 * f
+                    f = flags[oi - 1 : oi]
+                    low = jnp.broadcast_to((f - 1.0) * 199.0 - 1.0, (8, LANES))
+                    high = jnp.broadcast_to((f - 1.0) * 205.0 + 5.0, (8, LANES))
                 xs = jnp.broadcast_to(own[0:1] - dx * spacing * SCALE, (8, LANES))
                 ys = jnp.broadcast_to(own[1:2] - dy * spacing * SCALE, (8, LANES))
                 zs = jnp.broadcast_to(own[2:3], (8, LANES))
@@ -81,8 +81,8 @@
                     ddx = xs - cx
                     ddy = ys - cy
                     ddz = zs - cz
-                    t = -(ddx * ddx) - ddy * ddy - ddz * ddz
-                    w = f2 * jnp.exp2(4.0 * t) - fh * jnp.exp2(t)
+                    t = low - ddx * ddx - ddy * ddy - ddz * ddz
+                    w = jnp.exp2(4.0 * t + high) - jnp.exp2(t)
                     acc[0] = acc[0] + w * ddx
                     acc[1] = acc[1] + w * ddy
                     acc[2] = acc[2] + w * ddz

time: 133 us -> 131 us (0.985)
  Pallas kernels: 78.4 us -> 76.4 us
    pallas_call x1, Pallas kernels: 78.4 us -> 76.4 us  [cluster_forces(): pl.pallas_call(kernel, out_shape=jax.ShapeDtypeStruct((3, rows, width), j...]
where the time goes in v8:
time: 131 us
  Pallas kernels  76.4 us (58%)
  starting transfers between devices  27.9 us (21%)
  waiting for transfers between devices  20.3 us (15%)
  other arithmetic  2.43 us (2%)
  local copies, waits for them, and re-layouts  2.16 us (2%)
    pallas_call x1, Pallas kernels, cluster_forces(): pl.pallas_call(kernel, out_shape=jax.ShapeDtypeStruct((3, rows, width), j...  76.4 us
    ppermute x4, starting transfers between devices, passed_along(): lax.ppermute(value, axis, [(source, source + steps) for source in range(l...  17.1 us
    ppermute x3, waiting for transfers between devices, ring_shift(): lax.ppermute(value, axis, [(source, (source + steps) % count) for source...  16 us
    ppermute x3, starting transfers between devices, ring_shift(): lax.ppermute(value, axis, [(source, (source + steps) % count) for source...  10.8 us
    ppermute x4, waiting for transfers between devices, passed_along(): lax.ppermute(value, axis, [(source, source + steps) for source in range(l...  4.33 us
  transfers between devices with their start and end apart: 7, of which 4 were waited for; matrix products, arithmetic and copies ran while one was open for 1% of the time, Pallas kernels for 0%

profile of v8, /device:TPU:24, one launch (start us, length us, event | category | flops | bytes accessed | tf_op | source)
XLA Modules:
  0.0 130.6 jit_solution(15541904783007522724)
XLA Ops:
  0.6 0.0 copy-start
  0.6 1.3 %copy.11 = f32[1,3,16,2048]{3,1,2,0:T(4,128)S(1)} copy(f32[1,3,16,2048]{3,2,1,0:T(8,128)} %param.4) | data formatting | bytes 786432 | tf_op args[0]
  2.0 0.1 fusion.12
  2.1 1.9 %collective-permute-start.1 = (f32[3,16,64]{2,0,1:T(4,128)S(1)}, f32[3,16,64]{2,0,1:T(4,128)S(1)}, u32[]{:S(2)}, u32[]{:S(2)}) collective-permute-start(f32[3,16,64]{2,0,1:T(4,128)S(1)} %get-tuple-element.8), channel_id=1, source_target_pairs={{4,0},{8,4},{12,8},{16,12},{20,16},{24,20},{28,24},{5,1},{9,5},{13... | collective-permute-start | bytes 36872 | tf_op jit(solution)/shard_map/ppermute | solution.py:25
  4.0 2.4 %collective-permute-start = (f32[3,16,64]{2,0,1:T(4,128)S(1)}, f32[3,16,64]{2,0,1:T(4,128)S(1)}, u32[]{:S(2)}, u32[]{:S(2)}) collective-permute-start(f32[3,16,64]{2,0,1:T(4,128)S(1)} %get-tuple-element.9), channel_id=1, source_target_pairs={{0,4},{4,8},{8,12},{12,16},{16,20},{20,24},{24,28},{1,5},{5,9},{9,... | collective-permute-start | bytes 36872 | tf_op jit(solution)/shard_map/ppermute | solution.py:25
  6.4 0.0 copy-done
  6.4 0.3 multiply_bitcast_fusion.refs_0_
  6.8 0.0 collective-permute-done.1
  6.8 3.3 %collective-permute-done = f32[3,16,64]{2,0,1:T(4,128)S(1)} collective-permute-done((f32[3,16,64]{2,0,1:T(4,128)S(1)}, f32[3,16,64]{2,0,1:T(4,128)S(1)}, u32[]{:S(2)}, u32[]{:S(2)}) %collective-permute-start) | collective-permute-done | bytes 12320 | tf_op jit(solution)/shard_map/ppermute | solution.py:25
  10.1 0.7 concatenate.6
  10.8 0.0 copy-start.3
  10.9 4.5 %collective-permute-start.2 = (f32[3,1,2176]{2,0,1:T(4,128)S(1)}, f32[3,1,2176]{2,0,1:T(4,128)S(1)}, u32[]{:S(2)}, u32[]{:S(2)}) collective-permute-start(f32[3,1,2176]{2,0,1:T(4,128)S(1)} %get-tuple-element.6), channel_id=1, source_target_pairs={{0,32},{32,64},{64,96},{96,128},{128,160},{160,192},{192,224},{224... | collective-permute-start | bytes 78344 | tf_op jit(solution)/shard_map/ppermute | solution.py:25
  15.4 8.3 %collective-permute-start.3 = (f32[3,1,2176]{2,0,1:T(4,128)S(1)}, f32[3,1,2176]{2,0,1:T(4,128)S(1)}, u32[]{:S(2)}, u32[]{:S(2)}) collective-permute-start(f32[3,1,2176]{2,0,1:T(4,128)S(1)} %get-tuple-element.7), channel_id=1, source_target_pairs={{32,0},{64,32},{96,64},{128,96},{160,128},{192,160},{224,192},{256... | collective-permute-start | bytes 78344 | tf_op jit(solution)/shard_map/ppermute | solution.py:25
  23.7 0.0 copy-done.3
  23.7 0.6 convolution_bitcast_fusion.refs_2_
  24.2 0.0 collective-permute-done.2
  24.2 1.0 collective-permute-done.3
  25.2 0.2 fusion.refs_1_
  25.5 0.0 copy-start.1
  25.5 0.0 copy-start.2
  25.5 76.4 %shard_map.67 = f32[3,16,2048]{2,1,0:T(8,128)S(1)} custom-call(f32[16,3,2048]{2,1,0:T(4,128)S(1)} %multiply_bitcast_fusion.refs_0_, f32[18,3,2176]{2,1,0:T(4,128)S(1)} %fusion.refs_1_, f32[16,8,2048]{2,1,0:T(8,128)S(1)} %convolution_bitcast_fusion.refs_2_), custom_call_target="tpu_custom_call" | custom-call | flops 377487360 | bytes 2305024 | tf_op jit(solution)/shard_map/pallas_call | solution.py:110
  101.9 4.7 %collective-permute-start.6 = (f32[3,16,2048]{2,1,0:T(8,128)S(1)}, f32[3,16,2048]{2,1,0:T(8,128)S(1)}, u32[]{:S(2)}, u32[]{:S(2)}) collective-permute-start(f32[3,16,2048]{2,1,0:T(8,128)S(1)} %shard_map.67), channel_id=1, source_target_pairs={{0,3},{1,0},{2,1},{3,2},{4,7},{5,4},{6,5},{7,6},{8,11},{9,8},{10,9... | collective-permute-start | bytes 1179656 | tf_op jit(solution)/shard_map/ppermute | solution.py:30
  106.6 1.9 %collective-permute-start.5 = (f32[3,16,2048]{2,1,0:T(8,128)S(1)}, f32[3,16,2048]{2,1,0:T(8,128)S(1)}, u32[]{:S(2)}, u32[]{:S(2)}) collective-permute-start(f32[3,16,2048]{2,1,0:T(8,128)S(1)} %shard_map.67), channel_id=1, source_target_pairs={{0,1},{1,2},{2,3},{3,0},{4,5},{5,6},{6,7},{7,4},{8,9},{9,10},{10,1... | collective-permute-start | bytes 1179656 | tf_op jit(solution)/shard_map/ppermute | solution.py:30
  108.5 4.2 %collective-permute-start.4 = (f32[3,16,2048]{2,1,0:T(8,128)S(1)}, f32[3,16,2048]{2,1,0:T(8,128)S(1)}, u32[]{:S(2)}, u32[]{:S(2)}) collective-permute-start(f32[3,16,2048]{2,1,0:T(8,128)S(1)} %shard_map.67), channel_id=1, source_target_pairs={{0,2},{1,3},{2,0},{3,1},{4,6},{5,7},{6,4},{7,5},{8,10},{9,11},{10,... | collective-permute-start | bytes 1179656 | tf_op jit(solution)/shard_map/ppermute | solution.py:30
  112.7 10.7 %collective-permute-done.6 = f32[3,16,2048]{2,1,0:T(8,128)S(1)} collective-permute-done((f32[3,16,2048]{2,1,0:T(8,128)S(1)}, f32[3,16,2048]{2,1,0:T(8,128)S(1)}, u32[]{:S(2)}, u32[]{:S(2)}) %collective-permute-start.6) | collective-permute-done | bytes 393248 | tf_op jit(solution)/shard_map/ppermute | solution.py:30
  123.4 5.3 %collective-permute-done.5 = f32[3,16,2048]{2,1,0:T(8,128)S(1)} collective-permute-done((f32[3,16,2048]{2,1,0:T(8,128)S(1)}, f32[3,16,2048]{2,1,0:T(8,128)S(1)}, u32[]{:S(2)}, u32[]{:S(2)}) %collective-permute-start.5) | collective-permute-done | bytes 393248 | tf_op jit(solution)/shard_map/ppermute | solution.py:30
  128.7 0.0 collective-permute-done.4
  128.7 0.0 copy-done.1
  128.7 0.0 copy-done.2
  128.7 1.1 multiply_add_fusion
  129.8 0.8 broadcast_multiply_fusion
  (3 shorter events, 0.0 us)
Async XLA Ops:
  0.6 5.8 %copy-start = (f32[1,3,16,2048]{3,2,1,0:T(8,128)S(1)}, f32[1,3,16,2048]{3,2,1,0:T(8,128)}, u32[]{:S(2)}) copy-start(f32[1,3,16,2048]{3,2,1,0:T(8,128)} %param.4) | copy-start | bytes 1179652
  2.1 4.7 %collective-permute-start.1 = (f32[3,16,64]{2,0,1:T(4,128)S(1)}, f32[3,16,64]{2,0,1:T(4,128)S(1)}, u32[]{:S(2)}, u32[]{:S(2)}) collective-permute-start(f32[3,16,64]{2,0,1:T(4,128)S(1)} %get-tuple-element.8), channel_id=1, source_target_pairs={{4,0},{8,4},{12,8},{16,12},{20,16},{24,20},{28,24},{5,1},{9,5},{13... | collective-permute-start | bytes 36872 | tf_op jit(solution)/shard_map/ppermute | solution.py:25
  4.0 6.1 %collective-permute-start = (f32[3,16,64]{2,0,1:T(4,128)S(1)}, f32[3,16,64]{2,0,1:T(4,128)S(1)}, u32[]{:S(2)}, u32[]{:S(2)}) collective-permute-start(f32[3,16,64]{2,0,1:T(4,128)S(1)} %get-tuple-element.9), channel_id=1, source_target_pairs={{0,4},{4,8},{8,12},{12,16},{16,20},{20,24},{24,28},{1,5},{5,9},{9,... | collective-permute-start | bytes 36872 | tf_op jit(solution)/shard_map/ppermute | solution.py:25
  10.8 12.8 %copy-start.3 = (s32[16,32,8]{1,2,0:T(8,128)S(1)}, s32[16,32,8]{1,2,0:T(8,128)}, u32[]{:S(2)}) copy-start(s32[16,32,8]{1,2,0:T(8,128)} %param.7) | copy-start | bytes 49156
  10.9 13.4 %collective-permute-start.2 = (f32[3,1,2176]{2,0,1:T(4,128)S(1)}, f32[3,1,2176]{2,0,1:T(4,128)S(1)}, u32[]{:S(2)}, u32[]{:S(2)}) collective-permute-start(f32[3,1,2176]{2,0,1:T(4,128)S(1)} %get-tuple-element.6), channel_id=1, source_target_pairs={{0,32},{32,64},{64,96},{96,128},{128,160},{160,192},{192,224},{224... | collective-permute-start | bytes 78344 | tf_op jit(solution)/shard_map/ppermute | solution.py:25
  15.4 9.9 %collective-permute-start.3 = (f32[3,1,2176]{2,0,1:T(4,128)S(1)}, f32[3,1,2176]{2,0,1:T(4,128)S(1)}, u32[]{:S(2)}, u32[]{:S(2)}) collective-permute-start(f32[3,1,2176]{2,0,1:T(4,128)S(1)} %get-tuple-element.7), channel_id=1, source_target_pairs={{32,0},{64,32},{96,64},{128,96},{160,128},{192,160},{224,192},{256... | collective-permute-start | bytes 78344 | tf_op jit(solution)/shard_map/ppermute | solution.py:25
  25.5 103.2 %copy-start.1 = (f32[1,3,16,2048]{3,2,1,0:T(8,128)S(1)}, f32[1,3,16,2048]{3,2,1,0:T(8,128)}, u32[]{:S(2)}) copy-start(f32[1,3,16,2048]{3,2,1,0:T(8,128)} %param.6) | copy-start | bytes 1179652
  25.5 103.2 %copy-start.2 = (f32[1,3,16,2048]{3,2,1,0:T(8,128)S(1)}, f32[1,3,16,2048]{3,2,1,0:T(8,128)}, u32[]{:S(2)}) copy-start(f32[1,3,16,2048]{3,2,1,0:T(8,128)} %param.5) | copy-start | bytes 1179652
  101.9 21.5 %collective-permute-start.6 = (f32[3,16,2048]{2,1,0:T(8,128)S(1)}, f32[3,16,2048]{2,1,0:T(8,128)S(1)}, u32[]{:S(2)}, u32[]{:S(2)}) collective-permute-start(f32[3,16,2048]{2,1,0:T(8,128)S(1)} %shard_map.67), channel_id=1, source_target_pairs={{0,3},{1,0},{2,1},{3,2},{4,7},{5,4},{6,5},{7,6},{8,11},{9,8},{10,9... | collective-permute-start | bytes 1179656 | tf_op jit(solution)/shard_map/ppermute | solution.py:30
  106.6 22.1 %collective-permute-start.5 = (f32[3,16,2048]{2,1,0:T(8,128)S(1)}, f32[3,16,2048]{2,1,0:T(8,128)S(1)}, u32[]{:S(2)}, u32[]{:S(2)}) collective-permute-start(f32[3,16,2048]{2,1,0:T(8,128)S(1)} %shard_map.67), channel_id=1, source_target_pairs={{0,1},{1,2},{2,3},{3,0},{4,5},{5,6},{6,7},{7,4},{8,9},{9,10},{10,1... | collective-permute-start | bytes 1179656 | tf_op jit(solution)/shard_map/ppermute | solution.py:30
  108.5 20.2 %collective-permute-start.4 = (f32[3,16,2048]{2,1,0:T(8,128)S(1)}, f32[3,16,2048]{2,1,0:T(8,128)S(1)}, u32[]{:S(2)}, u32[]{:S(2)}) collective-permute-start(f32[3,16,2048]{2,1,0:T(8,128)S(1)} %shard_map.67), channel_id=1, source_target_pairs={{0,2},{1,3},{2,0},{3,1},{4,6},{5,7},{6,4},{7,5},{8,10},{9,11},{10,... | collective-permute-start | bytes 1179656 | tf_op jit(solution)/shard_map/ppermute | solution.py:30

commit v9 on v8

--- a/solution.py
+++ b/solution.py
@@ -141,11 +141,15 @@
               == lax.broadcasted_iota(jnp.int32, (cols_local, width), 0)).astype(jnp.float32)
     per_cluster = jnp.transpose(bonds.astype(jnp.float32), (0, 2, 1)).reshape(-1, cols_local)
     flags = jnp.dot(per_cluster, spread, precision=lax.Precision.HIGHEST).reshape(rows_local, -1, width)
-    force = cluster_forces(own, halo, flags)
-    across = ring_shift(force, "rep", 2)
-    near = ring_shift(force, "rep", 1)
-    far = ring_shift(force, "rep", 3)
-    summed_force = (force + across) + (near + far)
+    half = rows_local // 2
+    parts = []
+    for start, stop in ((0, half), (half, rows_local)):
+        force = cluster_forces(own[start:stop], halo[start : stop + 2], flags[start:stop])
+        across = ring_shift(force, "rep", 2)
+        near = ring_shift(force, "rep", 1)
+        far = ring_shift(force, "rep", 3)
+        parts.append((force + across) + (near + far))
+    summed_force = jnp.concatenate(parts, axis=1)
     mean_force = summed_force / lax.axis_size("rep")
     new_velocity = friction * velocities + time_step * mean_force[None] + noise_coef * noise
     new_position = positions + time_step * new_velocity

time: 131 us -> 134 us (1.023)
  the two profiles are of different devices: /device:TPU:24 before, /device:TPU:42 now
where the time goes in v9:
time: 134 us
  Pallas kernels  78.2 us (58%)
  starting transfers between devices  41 us (31%)
  waiting for transfers between devices  7.05 us (5%)
  local copies, waits for them, and re-layouts  3.75 us (3%)
  other arithmetic  2.44 us (2%)
    pallas_call x2, Pallas kernels, cluster_forces(): pl.pallas_call(kernel, out_shape=jax.ShapeDtypeStruct((3, rows, width), j...  78.2 us
    ppermute x4, starting transfers between devices, passed_along(): lax.ppermute(value, axis, [(source, source + steps) for source in range(l...  21.3 us
    ppermute x6, starting transfers between devices, ring_shift(): lax.ppermute(value, axis, [(source, (source + steps) % count) for source...  19.7 us
    ppermute x6, waiting for transfers between devices, ring_shift(): lax.ppermute(value, axis, [(source, (source + steps) % count) for source...  5.56 us
  transfers between devices with their start and end apart: 10, of which 3 were waited for; matrix products, arithmetic and copies ran while one was open for 1% of the time, Pallas kernels for 29%

profile of v9, /device:TPU:42, one launch (start us, length us, event | category | flops | bytes accessed | tf_op | source)
XLA Modules:
  0.0 133.9 jit_solution(2331897570077107600)
XLA Ops:
  0.6 1.3 copy.11
  1.9 0.0 copy-start.3
  1.9 0.1 fusion.15
  2.0 1.9 %collective-permute-start = (f32[3,16,64]{2,0,1:T(4,128)S(1)}, f32[3,16,64]{2,0,1:T(4,128)S(1)}, u32[]{:S(2)}, u32[]{:S(2)}) collective-permute-start(f32[3,16,64]{2,0,1:T(4,128)S(1)} %get-tuple-element.14), channel_id=1, source_target_pairs={{0,4},{4,8},{8,12},{12,16},{16,20},{20,24},{24,28},{1,5},{5,9},{9,... | collective-permute-start | bytes 36872 | tf_op jit(solution)/shard_map/ppermute | solution.py:25
  3.9 5.8 %collective-permute-start.1 = (f32[3,16,64]{2,0,1:T(4,128)S(1)}, f32[3,16,64]{2,0,1:T(4,128)S(1)}, u32[]{:S(2)}, u32[]{:S(2)}) collective-permute-start(f32[3,16,64]{2,0,1:T(4,128)S(1)} %get-tuple-element.13), channel_id=1, source_target_pairs={{4,0},{8,4},{12,8},{16,12},{20,16},{24,20},{28,24},{5,1},{9,5},{13... | collective-permute-start | bytes 36872 | tf_op jit(solution)/shard_map/ppermute | solution.py:25
  9.7 0.6 convolution_bitcast_fusion
  10.3 0.1 slice_bitcast_fusion.1
  10.4 0.9 copy-done
  11.3 0.3 multiply_bitcast_fusion
  11.6 0.7 concatenate.22
  12.4 4.3 %collective-permute-start.2 = (f32[3,1,2176]{2,0,1:T(4,128)S(1)}, f32[3,1,2176]{2,0,1:T(4,128)S(1)}, u32[]{:S(2)}, u32[]{:S(2)}) collective-permute-start(f32[3,1,2176]{2,0,1:T(4,128)S(1)} %get-tuple-element.9), channel_id=1, source_target_pairs={{0,32},{32,64},{64,96},{96,128},{128,160},{160,192},{192,224},{224... | collective-permute-start | bytes 78344 | tf_op jit(solution)/shard_map/ppermute | solution.py:25
  16.7 9.4 %collective-permute-start.3 = (f32[3,1,2176]{2,0,1:T(4,128)S(1)}, f32[3,1,2176]{2,0,1:T(4,128)S(1)}, u32[]{:S(2)}, u32[]{:S(2)}) collective-permute-start(f32[3,1,2176]{2,0,1:T(4,128)S(1)} %get-tuple-element.10), channel_id=1, source_target_pairs={{32,0},{64,32},{96,64},{128,96},{160,128},{192,160},{224,192},{256... | collective-permute-start | bytes 78344 | tf_op jit(solution)/shard_map/ppermute | solution.py:25
  26.1 0.1 fusion.14
  26.2 1.5 %collective-permute-done.3 = f32[3,1,2176]{2,0,1:T(4,128)S(1)} collective-permute-done((f32[3,1,2176]{2,0,1:T(4,128)S(1)}, f32[3,1,2176]{2,0,1:T(4,128)S(1)}, u32[]{:S(2)}, u32[]{:S(2)}) %collective-permute-start.3) | collective-permute-done | bytes 26144 | tf_op jit(solution)/shard_map/ppermute | solution.py:25
  27.7 0.2 fusion
  27.9 0.1 fusion.12
  28.0 39.1 %shard_map.67 = f32[3,8,2048]{2,1,0:T(8,128)S(1)} custom-call(f32[8,3,2048]{2,1,0:T(4,128)S(1)} %get-tuple-element.11.refs_0_, f32[10,3,2176]{2,1,0:T(4,128)S(1)} %get-tuple-element.7.refs_1_, f32[8,8,2048]{2,1,0:T(8,128)S(1)} %get-tuple-element.5.refs_2_), custom_call_target="tpu_custom_call" | custom-call | flops 188743680 | bytes 1178624 | tf_op jit(solution)/shard_map/pallas_call | solution.py:110
  67.1 4.0 %collective-permute-start.4 = (f32[3,8,2048]{2,1,0:T(8,128)S(1)}, f32[3,8,2048]{2,1,0:T(8,128)S(1)}, u32[]{:S(2)}, u32[]{:S(2)}) collective-permute-start(f32[3,8,2048]{2,1,0:T(8,128)S(1)} %shard_map.67), channel_id=1, source_target_pairs={{0,2},{1,3},{2,0},{3,1},{4,6},{5,7},{6,4},{7,5},{8,10},{9,11},{10,... | collective-permute-start | bytes 589832 | tf_op jit(solution)/shard_map/ppermute | solution.py:30
  71.1 1.9 %collective-permute-start.5 = (f32[3,8,2048]{2,1,0:T(8,128)S(1)}, f32[3,8,2048]{2,1,0:T(8,128)S(1)}, u32[]{:S(2)}, u32[]{:S(2)}) collective-permute-start(f32[3,8,2048]{2,1,0:T(8,128)S(1)} %shard_map.67), channel_id=1, source_target_pairs={{0,1},{1,2},{2,3},{3,0},{4,5},{5,6},{6,7},{7,4},{8,9},{9,10},{10,1... | collective-permute-start | bytes 589832 | tf_op jit(solution)/shard_map/ppermute | solution.py:30
  73.1 3.9 %collective-permute-start.6 = (f32[3,8,2048]{2,1,0:T(8,128)S(1)}, f32[3,8,2048]{2,1,0:T(8,128)S(1)}, u32[]{:S(2)}, u32[]{:S(2)}) collective-permute-start(f32[3,8,2048]{2,1,0:T(8,128)S(1)} %shard_map.67), channel_id=1, source_target_pairs={{0,3},{1,0},{2,1},{3,2},{4,7},{5,4},{6,5},{7,6},{8,11},{9,8},{10,9... | collective-permute-start | bytes 589832 | tf_op jit(solution)/shard_map/ppermute | solution.py:30
  77.0 39.1 %shard_map.68 = f32[3,8,2048]{2,1,0:T(8,128)S(1)} custom-call(f32[8,3,2048]{2,1,0:T(4,128)S(1)} %get-tuple-element.12.refs_0_, f32[10,3,2176]{2,1,0:T(4,128)S(1)} %get-tuple-element.8.refs_1_, f32[8,8,2048]{2,1,0:T(8,128)S(1)} %get-tuple-element.6.refs_2_), custom_call_target="tpu_custom_call" | custom-call | flops 188743680 | bytes 1178624 | tf_op jit(solution)/shard_map/pallas_call | solution.py:110
  116.1 3.4 %collective-permute-start.7 = (f32[3,8,2048]{2,1,0:T(8,128)S(1)}, f32[3,8,2048]{2,1,0:T(8,128)S(1)}, u32[]{:S(2)}, u32[]{:S(2)}) collective-permute-start(f32[3,8,2048]{2,1,0:T(8,128)S(1)} %shard_map.68), channel_id=1, source_target_pairs={{0,2},{1,3},{2,0},{3,1},{4,6},{5,7},{6,4},{7,5},{8,10},{9,11},{10,... | collective-permute-start | bytes 589832 | tf_op jit(solution)/shard_map/ppermute | solution.py:30
  119.5 4.5 %collective-permute-start.8 = (f32[3,8,2048]{2,1,0:T(8,128)S(1)}, f32[3,8,2048]{2,1,0:T(8,128)S(1)}, u32[]{:S(2)}, u32[]{:S(2)}) collective-permute-start(f32[3,8,2048]{2,1,0:T(8,128)S(1)} %shard_map.68), channel_id=1, source_target_pairs={{0,1},{1,2},{2,3},{3,0},{4,5},{5,6},{6,7},{7,4},{8,9},{9,10},{10,1... | collective-permute-start | bytes 589832 | tf_op jit(solution)/shard_map/ppermute | solution.py:30
  124.1 1.9 %collective-permute-start.9 = (f32[3,8,2048]{2,1,0:T(8,128)S(1)}, f32[3,8,2048]{2,1,0:T(8,128)S(1)}, u32[]{:S(2)}, u32[]{:S(2)}) collective-permute-start(f32[3,8,2048]{2,1,0:T(8,128)S(1)} %shard_map.68), channel_id=1, source_target_pairs={{0,3},{1,0},{2,1},{3,2},{4,7},{5,4},{6,5},{7,6},{8,11},{9,8},{10,9... | collective-permute-start | bytes 589832 | tf_op jit(solution)/shard_map/ppermute | solution.py:30
  126.0 0.1 add_add_fusion.1
  126.1 2.2 %collective-permute-done.8 = f32[3,8,2048]{2,1,0:T(8,128)S(1)} collective-permute-done((f32[3,8,2048]{2,1,0:T(8,128)S(1)}, f32[3,8,2048]{2,1,0:T(8,128)S(1)}, u32[]{:S(2)}, u32[]{:S(2)}) %collective-permute-start.8) | collective-permute-done | bytes 196640 | tf_op jit(solution)/shard_map/ppermute | solution.py:30
  128.3 3.4 %collective-permute-done.9 = f32[3,8,2048]{2,1,0:T(8,128)S(1)} collective-permute-done((f32[3,8,2048]{2,1,0:T(8,128)S(1)}, f32[3,8,2048]{2,1,0:T(8,128)S(1)}, u32[]{:S(2)}, u32[]{:S(2)}) %collective-permute-start.9) | collective-permute-done | bytes 196640 | tf_op jit(solution)/shard_map/ppermute | solution.py:30
  131.6 0.1 add_add_fusion
  131.7 0.8 maximum_multiply_fusion.1
  132.5 0.3 copy-done.1
  132.8 0.1 copy-done.2
  132.9 1.0 multiply_add_fusion
  (14 shorter events, 0.1 us)
Async XLA Ops:
  1.9 7.8 %copy-start.3 = (s32[16,32,8]{1,2,0:T(8,128)S(1)}, s32[16,32,8]{1,2,0:T(8,128)}, u32[]{:S(2)}) copy-start(s32[16,32,8]{1,2,0:T(8,128)} %param.7) | copy-start | bytes 49156
  2.0 9.6 %collective-permute-start = (f32[3,16,64]{2,0,1:T(4,128)S(1)}, f32[3,16,64]{2,0,1:T(4,128)S(1)}, u32[]{:S(2)}, u32[]{:S(2)}) collective-permute-start(f32[3,16,64]{2,0,1:T(4,128)S(1)} %get-tuple-element.14), channel_id=1, source_target_pairs={{0,4},{4,8},{8,12},{12,16},{16,20},{20,24},{24,28},{1,5},{5,9},{9,... | collective-permute-start | bytes 36872 | tf_op jit(solution)/shard_map/ppermute | solution.py:25
  3.9 7.7 %collective-permute-start.1 = (f32[3,16,64]{2,0,1:T(4,128)S(1)}, f32[3,16,64]{2,0,1:T(4,128)S(1)}, u32[]{:S(2)}, u32[]{:S(2)}) collective-permute-start(f32[3,16,64]{2,0,1:T(4,128)S(1)} %get-tuple-element.13), channel_id=1, source_target_pairs={{4,0},{8,4},{12,8},{16,12},{20,16},{24,20},{28,24},{5,1},{9,5},{13... | collective-permute-start | bytes 36872 | tf_op jit(solution)/shard_map/ppermute | solution.py:25
  10.3 1.0 copy-start
  12.4 13.8 %collective-permute-start.2 = (f32[3,1,2176]{2,0,1:T(4,128)S(1)}, f32[3,1,2176]{2,0,1:T(4,128)S(1)}, u32[]{:S(2)}, u32[]{:S(2)}) collective-permute-start(f32[3,1,2176]{2,0,1:T(4,128)S(1)} %get-tuple-element.9), channel_id=1, source_target_pairs={{0,32},{32,64},{64,96},{96,128},{128,160},{160,192},{192,224},{224... | collective-permute-start | bytes 78344 | tf_op jit(solution)/shard_map/ppermute | solution.py:25
  16.7 11.0 %collective-permute-start.3 = (f32[3,1,2176]{2,0,1:T(4,128)S(1)}, f32[3,1,2176]{2,0,1:T(4,128)S(1)}, u32[]{:S(2)}, u32[]{:S(2)}) collective-permute-start(f32[3,1,2176]{2,0,1:T(4,128)S(1)} %get-tuple-element.10), channel_id=1, source_target_pairs={{32,0},{64,32},{96,64},{128,96},{160,128},{192,160},{224,192},{256... | collective-permute-start | bytes 78344 | tf_op jit(solution)/shard_map/ppermute | solution.py:25
  67.1 57.0 %collective-permute-start.4 = (f32[3,8,2048]{2,1,0:T(8,128)S(1)}, f32[3,8,2048]{2,1,0:T(8,128)S(1)}, u32[]{:S(2)}, u32[]{:S(2)}) collective-permute-start(f32[3,8,2048]{2,1,0:T(8,128)S(1)} %shard_map.67), channel_id=1, source_target_pairs={{0,2},{1,3},{2,0},{3,1},{4,6},{5,7},{6,4},{7,5},{8,10},{9,11},{10,... | collective-permute-start | bytes 589832 | tf_op jit(solution)/shard_map/ppermute | solution.py:30
  71.1 54.9 %collective-permute-start.5 = (f32[3,8,2048]{2,1,0:T(8,128)S(1)}, f32[3,8,2048]{2,1,0:T(8,128)S(1)}, u32[]{:S(2)}, u32[]{:S(2)}) collective-permute-start(f32[3,8,2048]{2,1,0:T(8,128)S(1)} %shard_map.67), channel_id=1, source_target_pairs={{0,1},{1,2},{2,3},{3,0},{4,5},{5,6},{6,7},{7,4},{8,9},{9,10},{10,1... | collective-permute-start | bytes 589832 | tf_op jit(solution)/shard_map/ppermute | solution.py:30
  73.1 52.9 %collective-permute-start.6 = (f32[3,8,2048]{2,1,0:T(8,128)S(1)}, f32[3,8,2048]{2,1,0:T(8,128)S(1)}, u32[]{:S(2)}, u32[]{:S(2)}) collective-permute-start(f32[3,8,2048]{2,1,0:T(8,128)S(1)} %shard_map.67), channel_id=1, source_target_pairs={{0,3},{1,0},{2,1},{3,2},{4,7},{5,4},{6,5},{7,6},{8,11},{9,8},{10,9... | collective-permute-start | bytes 589832 | tf_op jit(solution)/shard_map/ppermute | solution.py:30
  116.1 10.0 %collective-permute-start.7 = (f32[3,8,2048]{2,1,0:T(8,128)S(1)}, f32[3,8,2048]{2,1,0:T(8,128)S(1)}, u32[]{:S(2)}, u32[]{:S(2)}) collective-permute-start(f32[3,8,2048]{2,1,0:T(8,128)S(1)} %shard_map.68), channel_id=1, source_target_pairs={{0,2},{1,3},{2,0},{3,1},{4,6},{5,7},{6,4},{7,5},{8,10},{9,11},{10,... | collective-permute-start | bytes 589832 | tf_op jit(solution)/shard_map/ppermute | solution.py:30
  119.5 8.8 %collective-permute-start.8 = (f32[3,8,2048]{2,1,0:T(8,128)S(1)}, f32[3,8,2048]{2,1,0:T(8,128)S(1)}, u32[]{:S(2)}, u32[]{:S(2)}) collective-permute-start(f32[3,8,2048]{2,1,0:T(8,128)S(1)} %shard_map.68), channel_id=1, source_target_pairs={{0,1},{1,2},{2,3},{3,0},{4,5},{5,6},{6,7},{7,4},{8,9},{9,10},{10,1... | collective-permute-start | bytes 589832 | tf_op jit(solution)/shard_map/ppermute | solution.py:30
  124.1 7.6 %collective-permute-start.9 = (f32[3,8,2048]{2,1,0:T(8,128)S(1)}, f32[3,8,2048]{2,1,0:T(8,128)S(1)}, u32[]{:S(2)}, u32[]{:S(2)}) collective-permute-start(f32[3,8,2048]{2,1,0:T(8,128)S(1)} %shard_map.68), channel_id=1, source_target_pairs={{0,3},{1,0},{2,1},{3,2},{4,7},{5,4},{6,5},{7,6},{8,11},{9,8},{10,9... | collective-permute-start | bytes 589832 | tf_op jit(solution)/shard_map/ppermute | solution.py:30
  131.7 1.1 copy-start.1
  131.7 1.2 copy-start.2
